TPU v7x, 32 devices: a whole 2x2x4 slice. The times are simulated.
32 devices in a mesh: groups: 2 (over y), cam: 4 (over z), tm: 2 (over x), chan: 2 (over core).
Axes of the slice: x: 2, y: 2, z: 4, core: 2. Of those that a mesh axis runs over, the one named last changes fastest.
Arguments:
- video: bfloat16 [16, 8, 16, 8, 256], P(('groups', 'cam'), 'tm', None, None, 'chan'), parts along dimension 0, may hold values from -6 to 6
- conv_weight: bfloat16 [27, 256, 256], P(None, None, 'chan'), may hold values from -0.078125 to 0.078125
- proj_weight: bfloat16 [256, 16], P('chan'), may hold values from -0.375 to 0.375
- rig_sizes: int32 [8], P('groups'), parts along dimension 0, may hold values from 1 to 3, as said below
- camera_order: int32 [16], P('groups'), parts along dimension 0, may hold values from 0 to 7, as said below
- owner_slot: int32 [8], P('groups'), parts along dimension 0, may hold values from 0 to 3, as said below
- cotangent: bfloat16 [8, 8, 16, 128], P(('groups', 'cam'), 'tm'), parts along dimension 0, may hold values from -6 to 6
Outputs:
- robot_latent: float32 [8, 8, 16, 128], P(('groups', 'cam'), 'tm'), parts along dimension 0
- grad_conv: bfloat16 [54, 256, 256], P('groups', None, 'chan'), parts along dimension 0
- grad_proj: float32 [512, 16], P(('groups', 'chan')), parts along dimension 0
- grad_video: bfloat16 [16, 8, 16, 8, 256], P(('groups', 'cam'), 'tm', None, None, 'chan'), parts along dimension 0
There are 2 independent parts, one for each index of `groups`. A program takes and returns all parts, laid end to end along the dimension named above; an argument that names none is the same for every part. Nothing has to cross between parts.
Inputs may be any that keep to these rules, and one draw needn't show every extreme that they name: `rig_sizes`: the sizes sum to 8; the largest is exactly 3. `camera_order`: A permutation; the cameras whose places fall from rig_sizes[0] + ... + rig_sizes[r-1] to below rig_sizes[0] + ... + rig_sizes[r] belong to robot r. `owner_slot`: A permutation of the output rows.
All inputs are finite; a program needn't handle non-finite values.
Results may differ from a plain program's by a relative error of at most 0.0059.
Values may be sent and summed in bfloat16 or wider, within the bound.
No kernel may reach another device: no remote copies, remote signals or barrier semaphores. Data moves between devices by JAX's collectives and lax.ppermute only.
A program may use at most 128 MiB of HBM per device.

v0:
```python
import jax
import jax.numpy as jnp
from jax import lax
from jax.sharding import PartitionSpec as P

KT = 3
KS = 3


def shifted(shard, axis, by):
    size = lax.axis_size(axis)
    pairs = [(i, i + by) for i in range(size) if 0 <= i + by < size]
    return lax.ppermute(shard, axis, pairs)


def tap_offsets():
    return [
        (shift_t, shift_h, shift_w)
        for shift_t in range(KT)
        for shift_h in range(KS)
        for shift_w in range(KS)
    ]


def forward_taps(extended, weight, frames, height, width):
    channels = extended.shape[-1]
    summed = jnp.zeros((extended.shape[0] * frames * height * width, weight.shape[2]), jnp.float32)
    for tap_index, (shift_t, shift_h, shift_w) in enumerate(tap_offsets()):
        window = extended[
            :, shift_t : shift_t + frames, shift_h : shift_h + height, shift_w : shift_w + width, :
        ].reshape(-1, channels)
        summed = summed + jnp.dot(window, weight[tap_index], preferred_element_type=jnp.float32)
    return summed


def weight_taps(extended, grad_rows, frames, height, width):
    channels = extended.shape[-1]
    results = []
    for shift_t, shift_h, shift_w in tap_offsets():
        window = extended[
            :, shift_t : shift_t + frames, shift_h : shift_h + height, shift_w : shift_w + width, :
        ].reshape(-1, channels)
        results.append(
            lax.dot_general(
                window, grad_rows, (((0,), (0,)), ((), ())), preferred_element_type=jnp.float32
            )
        )
    return jnp.stack(results)


def input_taps(grad_rows, weight, batch, frames, height, width):
    channels = weight.shape[1]
    pad_half = KS // 2
    padded = jnp.zeros(
        (batch, frames + KT - 1, height + KS - 1, width + KS - 1, channels), jnp.float32
    )
    for tap_index, (shift_t, shift_h, shift_w) in enumerate(tap_offsets()):
        backed = lax.dot_general(
            grad_rows,
            weight[tap_index],
            (((1,), (1,)), ((), ())),
            preferred_element_type=jnp.float32,
        )
        padded = padded.at[
            :, shift_t : shift_t + frames, shift_h : shift_h + height, shift_w : shift_w + width, :
        ].add(backed.reshape(batch, frames, height, width, channels))
    return padded[:, :, pad_half : pad_half + height, pad_half : pad_half + width, :]


def joining_matrix(rig_sizes, camera_order, owner_slot):
    robots = rig_sizes.shape[0]
    ends = jnp.cumsum(rig_sizes)
    robot_of = jnp.sum((ends[None, :] <= camera_order[:, None]).astype(jnp.int32), axis=1)
    member = robot_of[:, None] == jnp.arange(robots, dtype=jnp.int32)[None, :]
    slot_of = jnp.sum(jnp.where(member, owner_slot[None, :], 0), axis=1)
    count_of = jnp.sum(jnp.where(member, rig_sizes[None, :], 0), axis=1)
    share = 1.0 / count_of.astype(jnp.float32)
    placed = slot_of[None, :] == jnp.arange(robots, dtype=jnp.int32)[:, None]
    return jnp.where(placed, share[None, :], jnp.zeros_like(share)[None, :])


def body(video, conv_weight, proj_weight, rig_sizes, camera_order, owner_slot, cotangent):
    cam_dev, frames, height, width, half_chan = video.shape
    pad_half = KS // 2
    lat_width = proj_weight.shape[1]
    cache_half = shifted(video[:, frames - (KT - 1) :], "tm", 1)
    whole_now, whole_cache = (
        lax.all_gather(video, "chan", axis=4, tiled=True),
        lax.all_gather(cache_half, "chan", axis=4, tiled=True),
    )
    extended = jnp.concatenate([whole_cache, whole_now], axis=1)
    extended = jnp.pad(
        extended, ((0, 0), (0, 0), (pad_half, pad_half), (pad_half, pad_half), (0, 0))
    )
    pre = forward_taps(extended, conv_weight, frames, height, width)
    sigma = jax.nn.sigmoid(pre)
    act = (pre * sigma).astype(jnp.bfloat16)
    latent_part = jnp.dot(act, proj_weight, preferred_element_type=jnp.float32)
    latent = lax.psum(latent_part, "chan").astype(jnp.bfloat16)
    mixing = joining_matrix(rig_sizes, camera_order, owner_slot)
    cam_index = lax.axis_index("cam")
    my_row = lax.dynamic_slice_in_dim(mixing, cam_index, 1, 0)
    latent_maps = latent.reshape(cam_dev, frames, height, width * lat_width)
    block_in = lax.all_gather(latent_maps, "cam", axis=0, tiled=True)
    count_in = block_in.shape[0]
    flat_in = block_in.reshape(count_in, -1).astype(jnp.float32)
    added = jnp.dot(
        my_row, flat_in, precision=lax.Precision.HIGHEST, preferred_element_type=jnp.float32
    )
    robot_latent = added.reshape(
        jnp.zeros((1, frames, height, width * lat_width), jnp.float32).shape
    )
    my_cols = lax.dynamic_slice_in_dim(mixing, cam_index * cam_dev, cam_dev, 1)
    block_in = lax.all_gather(cotangent, "cam", axis=0, tiled=True)
    count_in = block_in.shape[0]
    flat_in = block_in.reshape(count_in, -1).astype(jnp.float32)
    spread = lax.dot_general(
        my_cols,
        flat_in,
        (((0,), (0,)), ((), ())),
        precision=lax.Precision.HIGHEST,
        preferred_element_type=jnp.float32,
    )
    dlatent = spread.astype(jnp.bfloat16).reshape(-1, lat_width)
    grad_proj_local = lax.dot_general(
        act, dlatent, (((0,), (0,)), ((), ())), preferred_element_type=jnp.float32
    )
    dact = lax.dot_general(
        dlatent, proj_weight, (((1,), (1,)), ((), ())), preferred_element_type=jnp.float32
    )
    dpre = (dact * sigma * (1.0 + pre * (1.0 - sigma))).astype(jnp.bfloat16)
    full_back = input_taps(dpre, conv_weight, cam_dev, frames, height, width)
    cache_part = full_back[:, : KT - 1]
    incoming = shifted(cache_part, "tm", -1)
    own_part = full_back[:, KT - 1 :]
    own_part = own_part.at[:, frames - (KT - 1) :].add(incoming)
    grad_conv_local = weight_taps(extended, dpre, frames, height, width)
    grad_conv, grad_proj = lax.psum((grad_conv_local, grad_proj_local), ("cam", "tm"))
    grad_video = lax.psum_scatter(
        own_part.astype(jnp.bfloat16), "chan", scatter_dimension=4, tiled=True
    )
    return (robot_latent, grad_conv.astype(jnp.bfloat16), grad_proj, grad_video)


def solution(mesh):
    return jax.shard_map(
        body,
        mesh=mesh,
        in_specs=(
            P(("groups", "cam"), "tm", None, None, "chan"),
            P(None, None, "chan"),
            P("chan", None),
            P("groups"),
            P("groups"),
            P("groups"),
            P(("groups", "cam"), "tm", None, None),
        ),
        out_specs=(
            P(("groups", "cam"), "tm", None, None),
            P("groups", None, "chan"),
            P(("groups", "chan"), None),
            P(("groups", "cam"), "tm", None, None, "chan"),
        ),
        check_vma=False,
    )
```

profile of v0, /device:TPU:0, one launch (start us, length us, event | category | flops | bytes accessed | tf_op | source)
XLA Modules:
  0.0 450.1 jit_solution(12302339504369722204)
XLA Ops:
  7.2 0.9 slice.1486
  8.2 4.8 %collective-permute-start = (bf16[2,2,16,8,128]{4,3,2,1,0:T(8,128)(2,1)S(1)}, bf16[2,2,16,8,128]{4,3,2,1,0:T(8,128)(2,1)S(1)}, u32[]{:S(2)}, u32[]{:S(2)}) collective-permute-start(bf16[2,2,16,8,128]{4,3,2,1,0:T(8,128)(2,1)S(1)} %slice.1486), channel_id=1, source_target_pairs={{0,2},{1,3},{4,6},{5,7},{8,10},{9,11},{12,14},{13,15},{16,18},{17,... | collective-permute-start | bytes 393224 | tf_op jit(solution)/shard_map/ppermute | solution.py:13
  13.0 0.8 reduce-window.8
  15.4 13.6 %all_gather.15 = bf16[4,4,16,128]{3,2,1,0:T(8,128)(2,1)S(1)} all-gather(bf16[1,4,16,128]{3,2,1,0:T(8,128)(2,1)} %param.69), channel_id=1, replica_groups=mesh['groups'=2,'cam'=4,'tm'=2,'chan'=2] {'cam'}, dimensions={0}, use_global_device_ids=true | all-gather | bytes 81920 | tf_op jit(solution)/shard_map/all_gather | solution.py:114
  30.2 2.4 all_gather.13
  32.5 2.0 all_gather.12
  35.0 2.3 pad_slice_fusion
  55.7 1.8 copy-done.3
  58.1 2.2 scatter-add.94
  60.3 6.7 %scatter-add.95 = f32[2,6,18,10,256]{4,3,2,1,0:T(8,128)} dynamic-update-slice(f32[2,6,18,10,256]{4,3,2,1,0:T(8,128)} %scatter-add.94, f32[2,4,16,8,256]{4,3,2,1,0:T(8,128)S(1)} %convolution_add_fusion.25, s32[]{:T(128)} %constant.917.clone.1, s32[]{:T(128)} %constant.917.clone.1, s32[]{:T(128)} %constant.917.clone.1, s32[]{:T(128)} %constant.926.clone.1, s32[]{:T(128)} %constant.917.clone.1) | dynamic-update-slice | bytes 2097156 | tf_op jit(solution)/shard_map/scatter-add | solution.py:66
  67.0 1.8 convolution_add_fusion.24
  68.9 6.7 %scatter-add.96 = f32[2,6,18,10,256]{4,3,2,1,0:T(8,128)} dynamic-update-slice(f32[2,6,18,10,256]{4,3,2,1,0:T(8,128)} %scatter-add.95, f32[2,4,16,8,256]{4,3,2,1,0:T(8,128)S(1)} %convolution_add_fusion.24, s32[]{:T(128)} %constant.917.clone.1, s32[]{:T(128)} %constant.917.clone.1, s32[]{:T(128)} %constant.917.clone.1, s32[]{:T(128)} %constant.924.clone.1, s32[]{:T(128)} %constant.917.clone.1) | dynamic-update-slice | bytes 2097156 | tf_op jit(solution)/shard_map/scatter-add | solution.py:66
  75.6 2.6 fusion.7
  78.1 1.8 convolution_add_fusion.22
  80.0 6.7 %scatter-add.100 = f32[2,6,18,10,256]{4,3,2,1,0:T(8,128)} dynamic-update-slice(f32[2,6,18,10,256]{4,3,2,1,0:T(8,128)} %fusion.7, f32[2,4,16,8,256]{4,3,2,1,0:T(8,128)S(1)} %convolution_add_fusion.22, s32[]{:T(128)} %constant.917.clone.1, s32[]{:T(128)} %constant.917.clone.1, s32[]{:T(128)} %constant.926.clone.1, s32[]{:T(128)} %constant.926.clone.1, s32[]{:T(128)} %constant.917.clone.1) | dynamic-update-slice | bytes 2097156 | tf_op jit(solution)/shard_map/scatter-add | solution.py:66
  86.7 3.8 convolution_add_fusion.21
  90.5 8.6 %scatter-add.101 = f32[2,6,18,10,256]{4,3,2,1,0:T(8,128)} dynamic-update-slice(f32[2,6,18,10,256]{4,3,2,1,0:T(8,128)} %scatter-add.100, f32[2,4,16,8,256]{4,3,2,1,0:T(8,128)S(1)} %convolution_add_fusion.21, s32[]{:T(128)} %constant.917.clone.1, s32[]{:T(128)} %bitcast.103, s32[]{:T(128)} %bitcast.104, s32[]{:T(128)} %bitcast.105, s32[]{:T(128)} %constant.917.clone.1) | dynamic-update-slice | bytes 2097156 | tf_op jit(solution)/shard_map/scatter-add | solution.py:66
  99.1 2.6 fusion.6
  101.8 1.9 convolution_add_fusion.19
  103.6 6.7 %scatter-add.105 = f32[2,6,18,10,256]{4,3,2,1,0:T(8,128)} dynamic-update-slice(f32[2,6,18,10,256]{4,3,2,1,0:T(8,128)} %fusion.6, f32[2,4,16,8,256]{4,3,2,1,0:T(8,128)S(1)} %convolution_add_fusion.19, s32[]{:T(128)} %constant.917.clone.1, s32[]{:T(128)} %constant.917.clone.1, s32[]{:T(128)} %constant.924.clone.1, s32[]{:T(128)} %constant.926.clone.1, s32[]{:T(128)} %constant.917.clone.1) | dynamic-update-slice | bytes 2097156 | tf_op jit(solution)/shard_map/scatter-add | solution.py:66
  110.3 1.9 convolution_add_fusion.18
  112.2 6.7 %scatter-add.106 = f32[2,6,18,10,256]{4,3,2,1,0:T(8,128)} dynamic-update-slice(f32[2,6,18,10,256]{4,3,2,1,0:T(8,128)} %scatter-add.105, f32[2,4,16,8,256]{4,3,2,1,0:T(8,128)S(1)} %convolution_add_fusion.18, s32[]{:T(128)} %constant.917.clone.1, s32[]{:T(128)} %constant.917.clone.1, s32[]{:T(128)} %constant.924.clone.1, s32[]{:T(128)} %constant.924.clone.1, s32[]{:T(128)} %constant.917.clone.1) | dynamic-update-slice | bytes 2097156 | tf_op jit(solution)/shard_map/scatter-add | solution.py:66
  118.9 2.7 fusion.5
  121.6 1.9 convolution_add_fusion.16
  123.4 6.8 %scatter-add.110 = f32[2,6,18,10,256]{4,3,2,1,0:T(8,128)} dynamic-update-slice(f32[2,6,18,10,256]{4,3,2,1,0:T(8,128)} %fusion.5, f32[2,4,16,8,256]{4,3,2,1,0:T(8,128)S(1)} %convolution_add_fusion.16, s32[]{:T(128)} %constant.917.clone.1, s32[]{:T(128)} %constant.926.clone.1, s32[]{:T(128)} %constant.917.clone.1, s32[]{:T(128)} %constant.926.clone.1, s32[]{:T(128)} %constant.917.clone.1) | dynamic-update-slice | bytes 2097156 | tf_op jit(solution)/shard_map/scatter-add | solution.py:66
  130.2 1.9 convolution_add_fusion.15
  132.1 6.8 %scatter-add.111 = f32[2,6,18,10,256]{4,3,2,1,0:T(8,128)} dynamic-update-slice(f32[2,6,18,10,256]{4,3,2,1,0:T(8,128)} %scatter-add.110, f32[2,4,16,8,256]{4,3,2,1,0:T(8,128)S(1)} %convolution_add_fusion.15, s32[]{:T(128)} %constant.917.clone.1, s32[]{:T(128)} %constant.926.clone.1, s32[]{:T(128)} %constant.917.clone.1, s32[]{:T(128)} %constant.924.clone.1, s32[]{:T(128)} %constant.917.clone.1) | dynamic-update-slice | bytes 2097156 | tf_op jit(solution)/shard_map/scatter-add | solution.py:66
  138.9 2.7 fusion.4
  141.5 1.9 convolution_add_fusion.13
  143.4 6.7 %scatter-add.115 = f32[2,6,18,10,256]{4,3,2,1,0:T(8,128)} dynamic-update-slice(f32[2,6,18,10,256]{4,3,2,1,0:T(8,128)} %fusion.4, f32[2,4,16,8,256]{4,3,2,1,0:T(8,128)S(1)} %convolution_add_fusion.13, s32[]{:T(128)} %constant.917.clone.1, s32[]{:T(128)} %constant.926.clone.1, s32[]{:T(128)} %constant.926.clone.1, s32[]{:T(128)} %constant.926.clone.1, s32[]{:T(128)} %constant.917.clone.1) | dynamic-update-slice | bytes 2097156 | tf_op jit(solution)/shard_map/scatter-add | solution.py:66
  150.1 1.9 convolution_add_fusion.12
  152.0 6.7 %scatter-add.116 = f32[2,6,18,10,256]{4,3,2,1,0:T(8,128)} dynamic-update-slice(f32[2,6,18,10,256]{4,3,2,1,0:T(8,128)} %scatter-add.115, f32[2,4,16,8,256]{4,3,2,1,0:T(8,128)S(1)} %convolution_add_fusion.12, s32[]{:T(128)} %constant.917.clone.1, s32[]{:T(128)} %constant.926.clone.1, s32[]{:T(128)} %constant.926.clone.1, s32[]{:T(128)} %constant.924.clone.1, s32[]{:T(128)} %constant.917.clone.1) | dynamic-update-slice | bytes 2097156 | tf_op jit(solution)/shard_map/scatter-add | solution.py:66
  158.8 2.7 fusion.3
  161.4 1.9 convolution_add_fusion.10
  163.3 6.7 %scatter-add.120 = f32[2,6,18,10,256]{4,3,2,1,0:T(8,128)} dynamic-update-slice(f32[2,6,18,10,256]{4,3,2,1,0:T(8,128)} %fusion.3, f32[2,4,16,8,256]{4,3,2,1,0:T(8,128)S(1)} %convolution_add_fusion.10, s32[]{:T(128)} %constant.917.clone.1, s32[]{:T(128)} %constant.926.clone.1, s32[]{:T(128)} %constant.924.clone.1, s32[]{:T(128)} %constant.926.clone.1, s32[]{:T(128)} %constant.917.clone.1) | dynamic-update-slice | bytes 2097156 | tf_op jit(solution)/shard_map/scatter-add | solution.py:66
  170.1 1.9 convolution_add_fusion.9
  172.0 6.7 %scatter-add.121 = f32[2,6,18,10,256]{4,3,2,1,0:T(8,128)} dynamic-update-slice(f32[2,6,18,10,256]{4,3,2,1,0:T(8,128)} %scatter-add.120, f32[2,4,16,8,256]{4,3,2,1,0:T(8,128)S(1)} %convolution_add_fusion.9, s32[]{:T(128)} %constant.917.clone.1, s32[]{:T(128)} %constant.926.clone.1, s32[]{:T(128)} %constant.924.clone.1, s32[]{:T(128)} %constant.924.clone.1, s32[]{:T(128)} %constant.917.clone.1) | dynamic-update-slice | bytes 2097156 | tf_op jit(solution)/shard_map/scatter-add | solution.py:66
  178.7 2.6 fusion.2
  181.3 1.9 convolution_add_fusion.7
  183.2 6.7 %scatter-add.125 = f32[2,6,18,10,256]{4,3,2,1,0:T(8,128)} dynamic-update-slice(f32[2,6,18,10,256]{4,3,2,1,0:T(8,128)} %fusion.2, f32[2,4,16,8,256]{4,3,2,1,0:T(8,128)S(1)} %convolution_add_fusion.7, s32[]{:T(128)} %constant.917.clone.1, s32[]{:T(128)} %constant.924.clone.1, s32[]{:T(128)} %constant.917.clone.1, s32[]{:T(128)} %constant.926.clone.1, s32[]{:T(128)} %constant.917.clone.1) | dynamic-update-slice | bytes 2097156 | tf_op jit(solution)/shard_map/scatter-add | solution.py:66
  189.9 1.9 convolution_add_fusion.6
  191.8 6.7 %scatter-add.126 = f32[2,6,18,10,256]{4,3,2,1,0:T(8,128)} dynamic-update-slice(f32[2,6,18,10,256]{4,3,2,1,0:T(8,128)} %scatter-add.125, f32[2,4,16,8,256]{4,3,2,1,0:T(8,128)S(1)} %convolution_add_fusion.6, s32[]{:T(128)} %constant.917.clone.1, s32[]{:T(128)} %constant.924.clone.1, s32[]{:T(128)} %constant.917.clone.1, s32[]{:T(128)} %constant.924.clone.1, s32[]{:T(128)} %constant.917.clone.1) | dynamic-update-slice | bytes 2097156 | tf_op jit(solution)/shard_map/scatter-add | solution.py:66
  198.5 2.6 fusion.1
  201.1 1.9 convolution_add_fusion.4
  203.0 7.0 %scatter-add.130 = f32[2,6,18,10,256]{4,3,2,1,0:T(8,128)} dynamic-update-slice(f32[2,6,18,10,256]{4,3,2,1,0:T(8,128)} %fusion.1, f32[2,4,16,8,256]{4,3,2,1,0:T(8,128)S(1)} %convolution_add_fusion.4, s32[]{:T(128)} %constant.917.clone.1, s32[]{:T(128)} %constant.924.clone.1, s32[]{:T(128)} %constant.926.clone.1, s32[]{:T(128)} %constant.926.clone.1, s32[]{:T(128)} %constant.917.clone.1) | dynamic-update-slice | bytes 2097156 | tf_op jit(solution)/shard_map/scatter-add | solution.py:66
  210.0 1.9 convolution_add_fusion.3
  211.9 6.7 %scatter-add.131 = f32[2,6,18,10,256]{4,3,2,1,0:T(8,128)} dynamic-update-slice(f32[2,6,18,10,256]{4,3,2,1,0:T(8,128)} %scatter-add.130, f32[2,4,16,8,256]{4,3,2,1,0:T(8,128)S(1)} %convolution_add_fusion.3, s32[]{:T(128)} %constant.917.clone.1, s32[]{:T(128)} %constant.924.clone.1, s32[]{:T(128)} %constant.926.clone.1, s32[]{:T(128)} %constant.924.clone.1, s32[]{:T(128)} %constant.917.clone.1) | dynamic-update-slice | bytes 2097156 | tf_op jit(solution)/shard_map/scatter-add | solution.py:66
  218.6 2.6 fusion
  221.2 1.9 convolution_add_fusion.1
  223.1 6.7 %scatter-add.135 = f32[2,6,18,10,256]{4,3,2,1,0:T(8,128)} dynamic-update-slice(f32[2,6,18,10,256]{4,3,2,1,0:T(8,128)} %fusion, f32[2,4,16,8,256]{4,3,2,1,0:T(8,128)S(1)} %convolution_add_fusion.1, s32[]{:T(128)} %constant.917.clone.1, s32[]{:T(128)} %constant.924.clone.1, s32[]{:T(128)} %constant.924.clone.1, s32[]{:T(128)} %constant.926.clone.1, s32[]{:T(128)} %constant.917.clone.1) | dynamic-update-slice | bytes 2097156 | tf_op jit(solution)/shard_map/scatter-add | solution.py:66
  229.8 1.9 convolution_add_fusion
  231.7 6.7 %scatter-add.136 = f32[2,6,18,10,256]{4,3,2,1,0:T(8,128)} dynamic-update-slice(f32[2,6,18,10,256]{4,3,2,1,0:T(8,128)} %scatter-add.135, f32[2,4,16,8,256]{4,3,2,1,0:T(8,128)S(1)} %convolution_add_fusion, s32[]{:T(128)} %constant.917.clone.1, s32[]{:T(128)} %constant.924.clone.1, s32[]{:T(128)} %constant.924.clone.1, s32[]{:T(128)} %constant.924.clone.1, s32[]{:T(128)} %constant.917.clone.1) | dynamic-update-slice | bytes 2097156 | tf_op jit(solution)/shard_map/scatter-add | solution.py:66
  238.4 1.3 slice.1599
  239.6 1.3 collective-permute-start.1
  240.9 3.6 psum.21
  244.6 1.7 slice.1597
  246.6 13.4 %all_gather.14 = bf16[8,4,16,128]{3,2,1,0:T(8,128)(2,1)S(1)} all-gather(bf16[2,4,16,128]{3,2,1,0:T(8,128)(2,1)S(1)} %reshape.1490), channel_id=1, replica_groups=mesh['groups'=2,'cam'=4,'tm'=2,'chan'=2] {'cam'}, dimensions={0}, use_global_device_ids=true | all-gather | bytes 163840 | tf_op jit(solution)/shard_map/all_gather | solution.py:104
  260.1 0.9 fusion.152
  261.2 1.4 fusion.37
  262.5 11.8 %copy.48 = bf16[2,4,16,8,256]{3,2,1,0,4:T(8,128)(2,1)} copy(bf16[2,4,16,8,256]{4,3,2,1,0:T(8,128)(2,1)S(1)} %fusion.37) | data formatting | bytes 1048576
  274.3 13.6 %reshape.1527 = bf16[256,1024]{1,0:T(8,128)(2,1)} reshape(bf16[256,2,4,16,8]{4,3,2,1,0:T(8,128)(2,1)} %bitcast.557) | data formatting | bytes 1048576
  288.0 142.3 %all-reduce.4 = (bf16[27,256,128]{2,1,0:T(8,128)(2,1)}, f32[128,16]{0,1:T(8,128)}) all-reduce(f32[27,256,128]{2,1,0:T(8,128)S(1)} %copy-done.4, f32[128,16]{0,1:T(8,128)S(1)} %fusion.156), channel_id=1, replica_groups=mesh['groups'=2,'cam'=4,'tm'=2,'chan'=2] {'cam','tm'}, use_global_device_ids=true, to_apply=%region_5.6 | all-reduce | flops 886784 | bytes 5324800 | tf_op jit(solution)/shard_map/psum | solution.py:138
  430.3 6.8 %reshape.1528 = bf16[128,2,4,16,8]{4,3,2,1,0:T(8,128)(2,1)} reshape(bf16[128,1024]{1,0:T(8,128)(2,1)} %reduce-scatter.4.cloned.1.call-done) | data formatting | bytes 524288
  437.2 6.1 %copy.49 = bf16[2,4,16,8,128]{4,3,2,1,0:T(8,128)(2,1)} copy(bf16[2,4,16,8,128]{3,2,1,0,4:T(8,128)(2,1)} %bitcast.558) | data formatting | bytes 524288
  (91 shorter events, 22.6 us)
Async XLA Ops:
  7.2 38.4 %copy-start = (bf16[128,16]{0,1:T(8,128)(2,1)S(1)}, bf16[128,16]{0,1:T(8,128)(2,1)}, u32[]{:S(2)}) copy-start(bf16[128,16]{0,1:T(8,128)(2,1)} %param.65) | copy-start | bytes 12292
  7.2 423.2 %reduce-scatter.4.cloned.1.call-start = ((), (), s32[]{:S(2)}) async-start(), calls=%async_computation.1 | async-start | bytes 786432
  8.2 24.4 %collective-permute-start = (bf16[2,2,16,8,128]{4,3,2,1,0:T(8,128)(2,1)S(1)}, bf16[2,2,16,8,128]{4,3,2,1,0:T(8,128)(2,1)S(1)}, u32[]{:S(2)}, u32[]{:S(2)}) collective-permute-start(bf16[2,2,16,8,128]{4,3,2,1,0:T(8,128)(2,1)S(1)} %slice.1486), channel_id=1, source_target_pairs={{0,2},{1,3},{4,6},{5,7},{8,10},{9,11},{12,14},{13,15},{16,18},{17,... | collective-permute-start | bytes 393224 | tf_op jit(solution)/shard_map/ppermute | solution.py:13
  35.0 2.3 copy-start.2
  45.6 2.2 copy-start.5
  55.7 1.8 copy-start.3
  229.8 31.2 %copy-start.6 = (bf16[1024,128]{1,0:T(8,128)(2,1)S(1)}, bf16[1024,128]{1,0:T(8,128)(2,1)}, u32[]{:S(2)}) copy-start(bf16[1024,128]{1,0:T(8,128)(2,1)} %copy-done.5) | copy-start | bytes 786436
  239.6 21.5 %collective-permute-start.1 = (f32[2,2,16,8,256]{4,3,2,1,0:T(8,128)S(1)}, f32[2,2,16,8,256]{4,3,2,1,0:T(8,128)S(1)}, u32[]{:S(2)}, u32[]{:S(2)}) collective-permute-start(f32[2,2,16,8,256]{4,3,2,1,0:T(8,128)S(1)} %slice.1599), channel_id=1, source_target_pairs={{2,0},{3,1},{6,4},{7,5},{10,8},{11,9},{14,12},{15,13},{18,16},{19,... | collective-permute-start | bytes 1572872 | tf_op jit(solution)/shard_map/ppermute | solution.py:13
  274.3 13.7 %copy-start.4 = (f32[27,256,128]{2,1,0:T(8,128)S(1)}, f32[27,256,128]{2,1,0:T(8,128)}, u32[]{:S(2)}) copy-start(f32[27,256,128]{2,1,0:T(8,128)} %copy-done.3) | copy-start | bytes 10616836
  288.0 155.3 %copy-start.1 = (bf16[128,16]{0,1:T(8,128)(2,1)S(1)}, bf16[128,16]{0,1:T(8,128)(2,1)}, u32[]{:S(2)}) copy-start(bf16[128,16]{0,1:T(8,128)(2,1)} %param.65) | copy-start | bytes 12292
Sparse Core Ops, SparseCore 0:
  288.1 10.2 reduce-scatter.3
where the time goes:
time: 454 us; the launch traced here: 450 us
  blocking collectives  177 us (39%)
  local copies, waits for them, and re-layouts  173 us (38%)
  matrix products  74.9 us (16%)
  between operations  14.6 us (3%)
  starting transfers between devices  6.18 us (1%)
    psum x1, blocking collectives, body(): lax.psum((grad_conv_local, grad_proj_local), ('cam', 'tm'))  142 us
    scatter-add x19, local copies, waits for them, and re-layouts, input_taps(): padded = padded.at[:, shift_t:shift_t + frames, shift_h:shift_h + height,...  125 us
    dot_general x27, matrix products, input_taps(): lax.dot_general(grad_rows, weight[tap_index], (((1,), (1,)), ((), ())), p...  55.4 us
    unnamed x20, local copies, waits for them, and re-layouts  40.4 us
    all_gather x1, blocking collectives, body(): block_in = lax.all_gather(cotangent, 'cam', axis=0, tiled=True)  13.6 us
    all_gather x1, blocking collectives, body(): block_in = lax.all_gather(latent_maps, 'cam', axis=0, tiled=True)  13.4 us
    dot_general x27, matrix products, weight_taps(): lax.dot_general(window, grad_rows, (((0,), (0,)), ((), ())), preferred_el...  9.49 us
  transfers between devices with their start and end apart: 3, of which 0 were waited for; matrix products, arithmetic and copies ran while one was open for 2% of the time, Pallas kernels for 0%

commit v1 on v0

v1 whole, which is shorter than its diff:
```python
import jax
import jax.numpy as jnp
from jax import lax
from jax.sharding import PartitionSpec as P

KT = 3
KS = 3


def shifted(shard, axis, by):
    size = lax.axis_size(axis)
    pairs = [(i, i + by) for i in range(size) if 0 <= i + by < size]
    return lax.ppermute(shard, axis, pairs)


def conv3d(lhs, rhs, padding, specs):
    return lax.conv_general_dilated(
        lhs,
        rhs,
        window_strides=(1, 1, 1),
        padding=padding,
        dimension_numbers=specs,
        preferred_element_type=jnp.float32,
    )


def joining_matrix(rig_sizes, camera_order, owner_slot):
    robots = rig_sizes.shape[0]
    ends = jnp.cumsum(rig_sizes)
    robot_of = jnp.sum((ends[None, :] <= camera_order[:, None]).astype(jnp.int32), axis=1)
    member = robot_of[:, None] == jnp.arange(robots, dtype=jnp.int32)[None, :]
    slot_of = jnp.sum(jnp.where(member, owner_slot[None, :], 0), axis=1)
    count_of = jnp.sum(jnp.where(member, rig_sizes[None, :], 0), axis=1)
    share = 1.0 / count_of.astype(jnp.float32)
    placed = slot_of[None, :] == jnp.arange(robots, dtype=jnp.int32)[:, None]
    return jnp.where(placed, share[None, :], jnp.zeros_like(share)[None, :])


def body(video, conv_weight, proj_weight, rig_sizes, camera_order, owner_slot, cotangent):
    cam_dev, frames, height, width, half_chan = video.shape
    pad_half = KS // 2
    lat_width = proj_weight.shape[1]
    out_half = conv_weight.shape[2]
    cache_half = shifted(video[:, frames - (KT - 1) :], "tm", 1)
    whole_now, whole_cache = (
        lax.all_gather(video, "chan", axis=4, tiled=True),
        lax.all_gather(cache_half, "chan", axis=4, tiled=True),
    )
    timed = jnp.concatenate([whole_cache, whole_now], axis=1)
    kernel = conv_weight.reshape(KT, KS, KS, conv_weight.shape[1], out_half)
    space_pad = [(0, 0), (pad_half, pad_half), (pad_half, pad_half)]
    pre5 = conv3d(timed, kernel, space_pad, ("NDHWC", "DHWIO", "NDHWC"))
    pre = pre5.reshape(-1, out_half)
    sigma = jax.nn.sigmoid(pre)
    act = (pre * sigma).astype(jnp.bfloat16)
    latent_part = jnp.dot(act, proj_weight, preferred_element_type=jnp.float32)
    latent = lax.psum(latent_part, "chan").astype(jnp.bfloat16)
    mixing = joining_matrix(rig_sizes, camera_order, owner_slot)
    cam_index = lax.axis_index("cam")
    my_row = lax.dynamic_slice_in_dim(mixing, cam_index, 1, 0)
    latent_maps = latent.reshape(cam_dev, frames, height, width * lat_width)
    block_in = lax.all_gather(latent_maps, "cam", axis=0, tiled=True)
    count_in = block_in.shape[0]
    flat_in = block_in.reshape(count_in, -1).astype(jnp.float32)
    added = jnp.dot(
        my_row, flat_in, precision=lax.Precision.HIGHEST, preferred_element_type=jnp.float32
    )
    robot_latent = added.reshape(1, frames, height, width * lat_width)
    my_cols = lax.dynamic_slice_in_dim(mixing, cam_index * cam_dev, cam_dev, 1)
    block_in = lax.all_gather(cotangent, "cam", axis=0, tiled=True)
    count_in = block_in.shape[0]
    flat_in = block_in.reshape(count_in, -1).astype(jnp.float32)
    spread = lax.dot_general(
        my_cols,
        flat_in,
        (((0,), (0,)), ((), ())),
        precision=lax.Precision.HIGHEST,
        preferred_element_type=jnp.float32,
    )
    dlatent = spread.astype(jnp.bfloat16).reshape(-1, lat_width)
    grad_proj_local = lax.dot_general(
        act, dlatent, (((0,), (0,)), ((), ())), preferred_element_type=jnp.float32
    )
    dact = lax.dot_general(
        dlatent, proj_weight, (((1,), (1,)), ((), ())), preferred_element_type=jnp.float32
    )
    dpre = (dact * sigma * (1.0 + pre * (1.0 - sigma))).astype(jnp.bfloat16)
    dpre5 = dpre.reshape(cam_dev, frames, height, width, out_half)
    grad_conv_local = conv3d(timed, dpre5, space_pad, ("CDHWN", "IDHWO", "DHWNC"))
    grad_conv_local = grad_conv_local.reshape(KT * KS * KS, -1, out_half)
    grad_conv_part = lax.psum_scatter(
        grad_conv_local, ("cam", "tm"), scatter_dimension=1, tiled=True
    )
    grad_proj = lax.psum(grad_proj_local, ("cam", "tm"))
    flipped = kernel[::-1, ::-1, ::-1]
    back_pad = [(KT - 1, KT - 1), (pad_half, pad_half), (pad_half, pad_half)]
    full_back = conv3d(dpre5, flipped, back_pad, ("NDHWC", "DHWOI", "NDHWC"))
    cache_part = full_back[:, : KT - 1]
    incoming = shifted(cache_part, "tm", -1)
    own_part = full_back[:, KT - 1 :]
    own_part = own_part.at[:, frames - (KT - 1) :].add(incoming)
    grad_video = lax.psum_scatter(
        own_part.astype(jnp.bfloat16), "chan", scatter_dimension=4, tiled=True
    )
    grad_conv = lax.all_gather(
        grad_conv_part.astype(jnp.bfloat16), ("cam", "tm"), axis=1, tiled=True
    )
    return (robot_latent, grad_conv, grad_proj, grad_video)


def solution(mesh):
    return jax.shard_map(
        body,
        mesh=mesh,
        in_specs=(
            P(("groups", "cam"), "tm", None, None, "chan"),
            P(None, None, "chan"),
            P("chan", None),
            P("groups"),
            P("groups"),
            P("groups"),
            P(("groups", "cam"), "tm", None, None),
        ),
        out_specs=(
            P(("groups", "cam"), "tm", None, None),
            P("groups", None, "chan"),
            P(("groups", "chan"), None),
            P(("groups", "cam"), "tm", None, None, "chan"),
        ),
        check_vma=False,
    )
```

time: 454 us -> 297 us (0.65)
  blocking collectives: 177 us -> 56.6 us
  matrix products: 74.9 us -> 27.1 us
  waiting for transfers between devices: 0.02 us -> 17.9 us
  local copies, waits for them, and re-layouts: 173 us -> 168 us
    unnamed x20 -> x24, local copies, waits for them, and re-layouts: 40.4 us -> 166 us
    scatter-add x19 -> x0, local copies, waits for them, and re-layouts: 125 us -> none  [input_taps(): padded = padded.at[:, shift_t:shift_t + frames, shift_h:shift_h + height,...]
    psum x1, blocking collectives: 142 us -> 21 us  [body(): grad_proj = lax.psum(grad_proj_local, ('cam', 'tm'))]
    dot_general x81 -> x0, matrix products: 73 us -> none  [the longest x27 55.4 us: input_taps(): lax.dot_general(grad_rows, weight[tap_index], (((1,), (1,)), ((), ())), p...]
    conv_general_dilated x0 -> x3, matrix products: none -> 24.7 us  [conv3d(): lax.conv_general_dilated(lhs, rhs, window_strides=(1, 1, 1), padding=padd...]
    ppermute x2, waiting for transfers between devices: 0.01 us -> 17.8 us  [shifted(): return lax.ppermute(shard, axis, pairs)]
  transfers between devices with their start and end apart: 3 -> 5, of which waited for: 0 -> 1; matrix products, arithmetic and copies ran while one was open for 2% -> 60% of each run, Pallas kernels for 0% -> 0%
where the time goes in v1:
time: 297 us; the launch traced here: 296 us
  local copies, waits for them, and re-layouts  168 us (57%)
  blocking collectives  56.6 us (19%)
  matrix products  27.1 us (9%)
  waiting for transfers between devices  17.9 us (6%)
  between operations  14 us (5%)
  starting transfers between devices  6.26 us (2%)
  other arithmetic  6.25 us (2%)
    unnamed x24, local copies, waits for them, and re-layouts  166 us
    conv_general_dilated x3, matrix products, conv3d(): lax.conv_general_dilated(lhs, rhs, window_strides=(1, 1, 1), padding=padd...  24.7 us
    psum x1, blocking collectives, body(): grad_proj = lax.psum(grad_proj_local, ('cam', 'tm'))  21 us
    ppermute x2, waiting for transfers between devices, shifted(): return lax.ppermute(shard, axis, pairs)  17.8 us
    all_gather x1, blocking collectives, body(): block_in = lax.all_gather(latent_maps, 'cam', axis=0, tiled=True)  14.2 us
    all_gather x1, blocking collectives, body(): block_in = lax.all_gather(cotangent, 'cam', axis=0, tiled=True)  13.6 us
    ppermute x2, starting transfers between devices, shifted(): return lax.ppermute(shard, axis, pairs)  6.14 us
  transfers between devices with their start and end apart: 5, of which 1 were waited for; matrix products, arithmetic and copies ran while one was open for 60% of the time, Pallas kernels for 0%

profile of v1, /device:TPU:0, one launch (start us, length us, event | category | flops | bytes accessed | tf_op | source)
XLA Modules:
  0.0 296.0 jit_solution(15450174119851827056)
XLA Ops:
  7.2 0.0 copy-start
  7.2 0.0 reduce-scatter.5.cloned.1.call-start
  7.2 1.3 copy.40
  8.6 0.1 slice.48
  8.7 4.8 %collective-permute-start = (bf16[2,2,16,8,128]{4,0,3,2,1:T(2,128)(2,1)S(1)}, bf16[2,2,16,8,128]{4,0,3,2,1:T(2,128)(2,1)S(1)}, u32[]{:S(2)}, u32[]{:S(2)}) collective-permute-start(bf16[2,2,16,8,128]{4,0,3,2,1:T(2,128)(2,1)S(1)} %slice.48), channel_id=1, source_target_pairs={{0,2},{1,3},{4,6},{5,7},{8,10},{9,11},{12,14},{13,15},{16,18},{17,... | collective-permute-start | bytes 393224 | tf_op jit(solution)/shard_map/ppermute | solution.py:13
  13.5 0.8 reduce-window.8
  14.4 0.7 convert_reduce_fusion
  15.1 0.8 select_reduce_fusion.1
  15.9 13.6 %all_gather.18 = bf16[4,4,16,128]{3,2,1,0:T(8,128)(2,1)S(1)} all-gather(bf16[1,4,16,128]{3,2,1,0:T(8,128)(2,1)} %param.15), channel_id=1, replica_groups=mesh['groups'=2,'cam'=4,'tm'=2,'chan'=2] {'cam'}, dimensions={0}, use_global_device_ids=true | all-gather | bytes 81920 | tf_op jit(solution)/shard_map/all_gather | solution.py:70
  29.5 0.0 copy-start.7
  29.5 0.5 copy-done.7
  30.0 0.4 convolution_convert_fusion
  30.4 0.2 reshape.128
  30.6 0.0 copy-start.1
  30.6 2.2 all_gather.16
  32.8 0.0 collective-permute-done
  32.8 2.0 all_gather.15
  34.8 0.2 constant_dynamic-update-slice_fusion.1
  35.0 0.5 constant_dynamic-update-slice_fusion
  35.5 0.0 copy-done
  35.5 6.6 %fusion.20 = f32[2,4,16,8,128]{4,0,3,2,1:T(2,128)S(1)} fusion(bf16[2,6,16,8,256]{4,0,3,2,1:T(2,128)(2,1)S(1)} %constant_dynamic-update-slice_fusion, bf16[3,3,3,256,128]{4,3,2,1,0:T(8,128)(2,1)S(1)} %bitcast.63), kind=kOutput, calls=%fused_computation.36 | convolution fusion | flops 1591738368 | bytes 3080192 | tf_op jit(solution)/shard_map/conv_general_dilated | solution.py:17
  42.1 0.0 copy-start.5
  42.1 0.9 multiply_convert_fusion
  43.0 0.9 fusion.5
  43.9 0.0 copy-done.1
  43.9 0.0 copy-done.5
  43.9 0.2 fusion.1
  44.1 10.6 %fusion.10 = f32[3,3,3,256,128]{4,3,2,1,0:T(8,128)} fusion(bf16[2,6,16,8,256]{4,0,3,2,1:T(2,128)(2,1)S(1)} %constant_dynamic-update-slice_fusion, bf16[2,4,16,8,128]{4,3,2,1,0:T(8,128)(2,1)S(1)} %bitcast.71), kind=kOutput, calls=%fused_computation.17 | convolution fusion | flops 1591738368 | bytes 4587520 | tf_op jit(solution)/shard_map/conv_general_dilated | solution.py:17
  54.7 0.0 reduce-scatter.5.cloned.1.call-update
  54.7 0.0 reduce-scatter.7.cloned.1.call-start
  54.8 7.5 %fusion.8 = f32[2,6,16,8,256]{4,0,3,2,1:T(2,128)S(1)} fusion(bf16[3,3,3,256,128]{4,3,2,1,0:T(8,128)(2,1)S(1)} %bitcast.64, bf16[2,4,16,8,128]{4,3,2,1,0:T(8,128)(2,1)S(1)} %bitcast.72), kind=kOutput, calls=%fused_computation.15 | convolution fusion | flops 1591738368 | bytes 3604480 | tf_op jit(solution)/shard_map/conv_general_dilated | solution.py:17
  62.3 0.2 slice.51
  62.5 1.3 collective-permute-start.1
  63.8 0.4 slice.49
  64.2 17.8 %collective-permute-done.1 = f32[2,2,16,8,256]{4,0,3,2,1:T(2,128)S(1)} collective-permute-done((f32[2,2,16,8,256]{4,0,3,2,1:T(2,128)S(1)}, f32[2,2,16,8,256]{4,0,3,2,1:T(2,128)S(1)}, u32[]{:S(2)}, u32[]{:S(2)}) %collective-permute-start.1) | collective-permute-done | bytes 524320 | tf_op jit(solution)/shard_map/ppermute | solution.py:13
  82.0 0.3 fusion.2
  82.3 51.9 %copy.51 = bf16[2,4,16,8,256]{0,3,2,1,4:T(8,128)(2,1)} copy(bf16[2,4,16,8,256]{4,0,3,2,1:T(2,128)(2,1)S(1)} %fusion.2) | data formatting | bytes 1048576
  134.2 0.0 copy-start.4
  134.2 0.0 copy-start.6
  134.2 49.8 %reshape.133 = bf16[256,1024]{1,0:T(8,128)(2,1)} reshape(bf16[256,4,16,8,2]{4,3,2,1,0:T(8,128)(2,1)} %bitcast.65) | data formatting | bytes 1048576
  183.9 0.0 copy-start.2
  183.9 0.0 copy-start.3
  183.9 0.0 reduce-scatter.7.cloned.1.call-update
  184.0 0.0 all-gather.2.cloned.1.call-start
  184.0 0.0 reduce-scatter.5.cloned.1.call-done
  184.0 1.8 convert_element_type.41
  185.8 0.0 all-gather.2.cloned.1.call-update
  185.9 0.0 copy-done.4
  185.9 0.0 copy-done.6
  185.9 0.2 fusion.21
  186.0 3.6 %psum.14 = bf16[1024,16]{0,1:T(8,128)(2,1)S(1)} all-reduce(f32[1024,16]{0,1:T(8,128)S(1)} %fusion.21), channel_id=1, replica_groups=mesh['groups'=2,'cam'=4,'tm'=2,'chan'=2] {'chan'}, use_global_device_ids=true, to_apply=%region_4.5 | all-reduce | flops 16384 | bytes 98304 | tf_op jit(solution)/shard_map/psum | solution.py:57
  189.7 0.2 copy.43
  189.8 0.2 reshape.124
  190.0 14.2 %all_gather.17 = bf16[8,4,16,128]{3,2,1,0:T(8,128)(2,1)S(1)} all-gather(bf16[2,4,16,128]{3,2,1,0:T(8,128)(2,1)S(1)} %reshape.124), channel_id=1, replica_groups=mesh['groups'=2,'cam'=4,'tm'=2,'chan'=2] {'cam'}, dimensions={0}, use_global_device_ids=true | all-gather | bytes 163840 | tf_op jit(solution)/shard_map/all_gather | solution.py:62
  204.2 0.1 copy.67
  204.3 0.0 copy-done.2
  204.4 0.0 copy-done.3
  204.4 0.2 fusion.22
  204.6 21.0 %psum.15 = f32[128,16]{0,1:T(8,128)} all-reduce(f32[128,16]{0,1:T(8,128)S(1)} %fusion.22), channel_id=1, replica_groups=mesh['groups'=2,'cam'=4,'tm'=2,'chan'=2] {'cam','tm'}, use_global_device_ids=true, to_apply=%region_6.7 | all-reduce | flops 2048 | bytes 16384 | tf_op jit(solution)/shard_map/psum | solution.py:94
  225.6 1.5 fusion.18
  227.1 0.0 reduce-scatter.7.cloned.1.call-done
  227.1 37.8 %reshape.134 = bf16[128,4,16,8,2]{4,3,2,1,0:T(8,128)(2,1)} reshape(bf16[128,1024]{1,0:T(8,128)(2,1)} %reduce-scatter.7.cloned.1.call-done) | data formatting | bytes 524288
  264.9 21.6 %copy.48 = bf16[2,4,16,8,128]{4,3,2,1,0:T(8,128)(2,1)} copy(bf16[2,4,16,8,128]{0,3,2,1,4:T(8,128)(2,1)} %bitcast.66) | data formatting | bytes 524288
  286.6 2.9 copy.71
  (3 shorter events, 0.0 us)
Async XLA Ops:
  7.2 28.3 %copy-start = (bf16[27,256,128]{2,1,0:T(8,128)(2,1)S(1)}, bf16[27,256,128]{2,1,0:T(8,128)(2,1)}, u32[]{:S(2)}) copy-start(bf16[27,256,128]{2,1,0:T(8,128)(2,1)} %param.10) | copy-start | bytes 5308420
  7.2 176.9 %reduce-scatter.5.cloned.1.call-start = ((), (), s32[]{:S(2)}) async-start(), calls=%async_computation.2 | async-start | bytes 3981312 | tf_op jit(solution)/shard_map/reduce_scatter | solution.py:91
  8.7 24.1 %collective-permute-start = (bf16[2,2,16,8,128]{4,0,3,2,1:T(2,128)(2,1)S(1)}, bf16[2,2,16,8,128]{4,0,3,2,1:T(2,128)(2,1)S(1)}, u32[]{:S(2)}, u32[]{:S(2)}) collective-permute-start(bf16[2,2,16,8,128]{4,0,3,2,1:T(2,128)(2,1)S(1)} %slice.48), channel_id=1, source_target_pairs={{0,2},{1,3},{4,6},{5,7},{8,10},{9,11},{12,14},{13,15},{16,18},{17,... | collective-permute-start | bytes 393224 | tf_op jit(solution)/shard_map/ppermute | solution.py:13
  29.5 0.5 copy-start.7
  30.6 13.3 %copy-start.1 = (bf16[1024,16]{1,0:T(8,128)(2,1)}, bf16[1024,16]{1,0:T(8,128)(2,1)S(1)}, u32[]{:S(2)}) copy-start(bf16[1024,16]{1,0:T(8,128)(2,1)S(1)} %reshape.128) | copy-start | bytes 98308
  42.1 1.8 copy-start.5
  54.7 172.4 %reduce-scatter.7.cloned.1.call-start = ((), (), s32[]{:S(2)}) async-start(), calls=%async_computation.4 | async-start | bytes 786432
  62.5 19.5 %collective-permute-start.1 = (f32[2,2,16,8,256]{4,0,3,2,1:T(2,128)S(1)}, f32[2,2,16,8,256]{4,0,3,2,1:T(2,128)S(1)}, u32[]{:S(2)}, u32[]{:S(2)}) collective-permute-start(f32[2,2,16,8,256]{4,0,3,2,1:T(2,128)S(1)} %slice.51), channel_id=1, source_target_pairs={{2,0},{3,1},{6,4},{7,5},{10,8},{11,9},{14,12},{15,13},{18,16},{19,... | collective-permute-start | bytes 1572872 | tf_op jit(solution)/shard_map/ppermute | solution.py:13
  134.2 51.7 %copy-start.4 = (bf16[1024,128]{1,0:T(8,128)(2,1)S(1)}, bf16[1024,128]{1,0:T(8,128)(2,1)}, u32[]{:S(2)}) copy-start(bf16[1024,128]{1,0:T(8,128)(2,1)} %get-tuple-element.41) | copy-start | bytes 786436
  134.2 51.7 %copy-start.6 = (bf16[128,16]{0,1:T(8,128)(2,1)S(1)}, bf16[128,16]{0,1:T(8,128)(2,1)}, u32[]{:S(2)}) copy-start(bf16[128,16]{0,1:T(8,128)(2,1)} %param.11) | copy-start | bytes 12292
  183.9 20.4 %copy-start.2 = (bf16[1024,16]{1,0:T(8,128)(2,1)S(1)}, bf16[1024,16]{1,0:T(8,128)(2,1)}, u32[]{:S(2)}) copy-start(bf16[1024,16]{1,0:T(8,128)(2,1)} %copy-done.1) | copy-start | bytes 98308
  183.9 20.4 %copy-start.3 = (bf16[2,4,16,8,128]{4,3,2,1,0:T(8,128)(2,1)S(1)}, bf16[2,4,16,8,128]{4,3,2,1,0:T(8,128)(2,1)}, u32[]{:S(2)}) copy-start(bf16[2,4,16,8,128]{4,3,2,1,0:T(8,128)(2,1)} %get-tuple-element.38) | copy-start | bytes 786436
  184.0 102.6 %all-gather.2.cloned.1.call-start = ((), (), s32[]{:S(2)}) async-start(), calls=%async_computation.3 | async-start | bytes 1990656 | tf_op jit(solution)/shard_map/all_gather | solution.py:105
Sparse Core Ops, SparseCore 0:
  54.8 79.9 reduce-scatter.4
  184.1 9.1 reduce-scatter.6
  195.5 48.6 all-gather.1

commit v2 on v1

--- a/solution.py
+++ b/solution.py
@@ -57,19 +57,18 @@
     latent = lax.psum(latent_part, "chan").astype(jnp.bfloat16)
     mixing = joining_matrix(rig_sizes, camera_order, owner_slot)
     cam_index = lax.axis_index("cam")
+    cam_count = lax.axis_size("cam")
     my_row = lax.dynamic_slice_in_dim(mixing, cam_index, 1, 0)
     latent_maps = latent.reshape(cam_dev, frames, height, width * lat_width)
-    block_in = lax.all_gather(latent_maps, "cam", axis=0, tiled=True)
-    count_in = block_in.shape[0]
-    flat_in = block_in.reshape(count_in, -1).astype(jnp.float32)
+    both = jnp.concatenate([latent_maps, cotangent], axis=0)
+    both_in = lax.all_gather(both, "cam", axis=0, tiled=False)
+    flat_in = both_in[:, :cam_dev].reshape(cam_count * cam_dev, -1).astype(jnp.float32)
     added = jnp.dot(
         my_row, flat_in, precision=lax.Precision.HIGHEST, preferred_element_type=jnp.float32
     )
     robot_latent = added.reshape(1, frames, height, width * lat_width)
     my_cols = lax.dynamic_slice_in_dim(mixing, cam_index * cam_dev, cam_dev, 1)
-    block_in = lax.all_gather(cotangent, "cam", axis=0, tiled=True)
-    count_in = block_in.shape[0]
-    flat_in = block_in.reshape(count_in, -1).astype(jnp.float32)
+    flat_in = both_in[:, cam_dev:].reshape(cam_count * cotangent.shape[0], -1).astype(jnp.float32)
     spread = lax.dot_general(
         my_cols,
         flat_in,
@@ -93,15 +92,26 @@
     )
     grad_proj = lax.psum(grad_proj_local, ("cam", "tm"))
     flipped = kernel[::-1, ::-1, ::-1]
-    back_pad = [(KT - 1, KT - 1), (pad_half, pad_half), (pad_half, pad_half)]
-    full_back = conv3d(dpre5, flipped, back_pad, ("NDHWC", "DHWOI", "NDHWC"))
-    cache_part = full_back[:, : KT - 1]
+    back_specs = ("NDHWC", "DHWOI", "NDHWC")
+    head_pad = [(KT - 1, 0), (pad_half, pad_half), (pad_half, pad_half)]
+    cache_part = conv3d(dpre5[:, : KT - 1], flipped, head_pad, back_specs)
     incoming = shifted(cache_part, "tm", -1)
-    own_part = full_back[:, KT - 1 :]
+    tail_pad = [(0, KT - 1), (pad_half, pad_half), (pad_half, pad_half)]
+    own_part = conv3d(dpre5, flipped, tail_pad, back_specs)
     own_part = own_part.at[:, frames - (KT - 1) :].add(incoming)
-    grad_video = lax.psum_scatter(
-        own_part.astype(jnp.bfloat16), "chan", scatter_dimension=4, tiled=True
+    rounded = own_part.astype(jnp.bfloat16)
+    chan_count = lax.axis_size("chan")
+    chan_index = lax.axis_index("chan")
+    width_out = rounded.shape[4] // chan_count
+    summed = lax.dynamic_slice_in_dim(rounded, chan_index * width_out, width_out, 4).astype(
+        jnp.float32
     )
+    for step in range(1, chan_count):
+        target = (chan_index + step) % chan_count
+        sent = lax.dynamic_slice_in_dim(rounded, target * width_out, width_out, 4)
+        pairs = [(i, (i + step) % chan_count) for i in range(chan_count)]
+        summed = summed + lax.ppermute(sent, "chan", pairs).astype(jnp.float32)
+    grad_video = summed.astype(jnp.bfloat16)
     grad_conv = lax.all_gather(
         grad_conv_part.astype(jnp.bfloat16), ("cam", "tm"), axis=1, tiled=True
     )

time: 297 us -> 201 us (0.68)
  local copies, waits for them, and re-layouts: 168 us -> 8.29 us
  waiting for transfers between devices: 17.9 us -> 95.2 us
  blocking collectives: 56.6 us -> 41.5 us
    unnamed x24 -> x14, local copies, waits for them, and re-layouts: 166 us -> 5.17 us
    reduce_scatter x1, waiting for transfers between devices: 0.02 us -> 80.1 us  [body(): lax.psum_scatter(grad_conv_local, ('cam', 'tm'), scatter_dimension=1, til...]
    all_gather x2 -> x1, blocking collectives: 27.8 us -> 14 us  [body(): both_in = lax.all_gather(both, 'cam', axis=0, tiled=False)]
    ppermute x2, waiting for transfers between devices: 17.8 us -> 11.3 us  [shifted(): return lax.ppermute(shard, axis, pairs)]
    all_gather x1, waiting for transfers between devices: 0.01 us -> 3.7 us  [body(): lax.all_gather(grad_conv_part.astype(jnp.bfloat16), ('cam', 'tm'), axis=1...]
    conv_general_dilated x3 -> x4, matrix products: 24.7 us -> 27.1 us  [conv3d(): lax.conv_general_dilated(lhs, rhs, window_strides=(1, 1, 1), padding=padd...]
  transfers between devices with their start and end apart: 5 -> 5, of which waited for: 1 -> 3; matrix products, arithmetic and copies ran while one was open for 60% -> 8% of each run, Pallas kernels for 0% -> 0%
where the time goes in v2:
time: 201 us
  waiting for transfers between devices  95.2 us (47%)
  blocking collectives  41.5 us (21%)
  matrix products  28.9 us (14%)
  between operations  14.3 us (7%)
  local copies, waits for them, and re-layouts  8.29 us (4%)
  starting transfers between devices  6.51 us (3%)
  other arithmetic  6.14 us (3%)
    reduce_scatter x1, waiting for transfers between devices, body(): lax.psum_scatter(grad_conv_local, ('cam', 'tm'), scatter_dimension=1, til...  80.1 us
    conv_general_dilated x4, matrix products, conv3d(): lax.conv_general_dilated(lhs, rhs, window_strides=(1, 1, 1), padding=padd...  27.1 us
    psum x1, blocking collectives, body(): grad_proj = lax.psum(grad_proj_local, ('cam', 'tm'))  19.7 us
    all_gather x1, blocking collectives, body(): both_in = lax.all_gather(both, 'cam', axis=0, tiled=False)  14 us
    ppermute x2, waiting for transfers between devices, shifted(): return lax.ppermute(shard, axis, pairs)  11.3 us
    ppermute x2, starting transfers between devices, shifted(): return lax.ppermute(shard, axis, pairs)  6.14 us
    unnamed x14, local copies, waits for them, and re-layouts  5.17 us
  transfers between devices with their start and end apart: 5, of which 3 were waited for; matrix products, arithmetic and copies ran while one was open for 8% of the time, Pallas kernels for 0%

profile of v2, /device:TPU:0, one launch (start us, length us, event | category | flops | bytes accessed | tf_op | source)
XLA Modules:
  0.0 200.9 jit_solution(11271773121406008095)
XLA Ops:
  7.2 0.0 copy-start
  7.2 0.0 copy-start.1
  7.2 0.0 reduce-scatter.2.cloned.1.call-start
  7.2 1.3 copy.44
  8.6 0.1 slice.51
  8.7 4.8 %collective-permute-start = (bf16[2,2,16,8,128]{4,0,3,2,1:T(2,128)(2,1)S(1)}, bf16[2,2,16,8,128]{4,0,3,2,1:T(2,128)(2,1)S(1)}, u32[]{:S(2)}, u32[]{:S(2)}) collective-permute-start(bf16[2,2,16,8,128]{4,0,3,2,1:T(2,128)(2,1)S(1)} %slice.51), channel_id=1, source_target_pairs={{0,2},{1,3},{4,6},{5,7},{8,10},{9,11},{12,14},{13,15},{16,18},{17,... | collective-permute-start | bytes 393224 | tf_op jit(solution)/shard_map/ppermute | solution.py:13
  13.5 0.8 reduce-window.8
  14.4 0.7 convert_reduce_fusion
  15.1 0.8 select_reduce_fusion.1
  15.9 2.2 %all_gather.16 = bf16[2,4,16,8,256]{4,0,3,2,1:T(2,128)(2,1)S(1)} all-gather(bf16[2,4,16,8,128]{4,0,3,2,1:T(2,128)(2,1)S(1)} %copy.44), channel_id=1, replica_groups=mesh['groups'=2,'cam'=4,'tm'=2,'chan'=2] {'chan'}, dimensions={4}, use_global_device_ids=true | all-gather | bytes 786432 | tf_op jit(solution)/shard_map/all_gather | solution.py:46
  18.1 0.0 collective-permute-done
  18.1 2.0 all_gather.15
  20.1 0.2 constant_dynamic-update-slice_fusion.1
  20.2 0.5 constant_dynamic-update-slice_fusion
  20.8 0.0 copy-start.3
  20.8 0.0 copy-done.1
  20.8 6.5 %fusion.22 = f32[2,4,16,8,128]{4,0,3,2,1:T(2,128)S(1)} fusion(bf16[2,6,16,8,256]{4,0,3,2,1:T(2,128)(2,1)S(1)} %constant_dynamic-update-slice_fusion, bf16[3,3,3,256,128]{4,3,2,1,0:T(8,128)(2,1)S(1)} %bitcast.58), kind=kOutput, calls=%fused_computation.40 | convolution fusion | flops 1591738368 | bytes 3080192 | tf_op jit(solution)/shard_map/conv_general_dilated | solution.py:17
  27.3 0.0 copy-done.3
  27.3 0.0 copy-start.4
  27.3 0.9 multiply_convert_fusion
  28.2 0.2 fusion.5
  28.4 0.0 copy-done
  28.4 0.2 fusion.23
  28.6 3.6 %psum.14 = bf16[1024,16]{0,1:T(8,128)(2,1)S(1)} all-reduce(f32[1024,16]{0,1:T(8,128)S(1)} %fusion.23), channel_id=1, replica_groups=mesh['groups'=2,'cam'=4,'tm'=2,'chan'=2] {'chan'}, use_global_device_ids=true, to_apply=%region_4.5 | all-reduce | flops 16384 | bytes 98304 | tf_op jit(solution)/shard_map/psum | solution.py:57
  32.2 0.2 copy.47
  32.4 0.2 reshape.124
  32.6 0.0 copy-done.4
  32.6 14.0 %all-gather = bf16[12,4,16,128]{3,2,1,0:T(8,128)(2,1)S(1)} all-gather(bf16[3,4,16,128]{3,2,1,0:T(8,128)(2,1)S(1)} %pad_maximum_fusion), channel_id=2, replica_groups=mesh['groups'=2,'cam'=4,'tm'=2,'chan'=2] {'cam'}, dimensions={0}, use_global_device_ids=true | all-gather | bytes 245760 | tf_op jit(solution)/shard_map/all_gather | solution.py:64
  46.6 0.4 convolution_convert_fusion
  47.0 0.2 reshape.128
  47.2 0.2 fusion.1
  47.4 11.5 %fusion.20 = f32[3,3,3,256,128]{4,3,2,1,0:T(8,128)} fusion(bf16[2,6,16,8,256]{4,0,3,2,1:T(2,128)(2,1)} %copy-done.3, bf16[2,4,16,8,128]{4,3,2,1,0:T(8,128)(2,1)S(1)} %bitcast.62), kind=kOutput, calls=%fused_computation.38 | convolution fusion | flops 1591738368 | bytes 4587520 | tf_op jit(solution)/shard_map/conv_general_dilated | solution.py:17
  59.0 0.0 reduce-scatter.2.cloned.1.call-update
  59.0 0.3 all-gather.3.cloned.1.call-start
  59.3 80.1 %reduce-scatter.2.cloned.1.call-done = f32[27,32,128]{2,1,0:T(8,128)} async-done(((f32[27,256,128]{2,1,0:T(8,128)}), f32[27,32,128]{2,1,0:T(8,128)}) %reduce-scatter.2.cloned.1.call-update) | async-done | bytes 442384 | tf_op jit(solution)/shard_map/reduce_scatter | solution.py:90
  139.3 1.7 convert_element_type.50
  141.1 0.0 all-gather.3.cloned.1.call-update
  141.1 1.4 rev.3
  142.5 0.3 copy.48
  142.8 4.1 %fusion.8 = f32[2,2,16,8,256]{4,0,3,2,1:T(2,128)S(1)} fusion(bf16[3,3,3,256,128]{4,3,2,1,0:T(8,128)(2,1)} %rev.3, bf16[2,4,16,8,128]{4,0,3,2,1:T(2,128)(2,1)S(1)} %copy.48), kind=kOutput, calls=%fused_computation.16 | convolution fusion | flops 397934592 | bytes 2424832 | tf_op jit(solution)/shard_map/conv_general_dilated | solution.py:17
  146.9 1.3 collective-permute-start.1
  148.2 5.0 %fusion.18 = f32[2,4,16,8,256]{4,0,3,2,1:T(2,128)S(1)} fusion(bf16[3,3,3,256,128]{4,3,2,1,0:T(8,128)(2,1)S(1)} %bitcast.60, bf16[2,4,16,8,128]{4,3,2,1,0:T(8,128)(2,1)S(1)} %bitcast.64), kind=kOutput, calls=%fused_computation.36 | convolution fusion | flops 1193803776 | bytes 3080192 | tf_op jit(solution)/shard_map/conv_general_dilated | solution.py:17
  153.1 0.0 copy-start.2
  153.2 11.3 %collective-permute-done.1 = f32[2,2,16,8,256]{4,0,3,2,1:T(2,128)S(1)} collective-permute-done((f32[2,2,16,8,256]{4,0,3,2,1:T(2,128)S(1)}, f32[2,2,16,8,256]{4,0,3,2,1:T(2,128)S(1)}, u32[]{:S(2)}, u32[]{:S(2)}) %collective-permute-start.1) | collective-permute-done | bytes 524320 | tf_op jit(solution)/shard_map/ppermute | solution.py:13
  164.5 0.3 fusion.2
  164.8 0.4 convert_element_type.53
  165.2 0.2 constant_dynamic-slice_fusion
  165.4 0.1 collective-permute-start.2
  165.5 0.0 copy-done.2
  165.5 0.2 fusion.24
  165.8 0.1 reshape.125
  165.8 19.7 %psum.15 = f32[128,16]{0,1:T(8,128)} all-reduce(f32[128,16]{0,1:T(8,128)S(1)} %fusion.24), channel_id=1, replica_groups=mesh['groups'=2,'cam'=4,'tm'=2,'chan'=2] {'cam','tm'}, use_global_device_ids=true, to_apply=%region_6.7 | all-reduce | flops 2048 | bytes 16384 | tf_op jit(solution)/shard_map/psum | solution.py:93
  185.6 0.9 fusion.16
  186.4 0.0 collective-permute-done.2
  186.4 0.3 add_convert_fusion
  186.7 0.7 copy.53
  187.5 3.7 %all-gather.3.cloned.1.call-done = bf16[27,256,128]{2,1,0:T(8,128)(2,1)} async-done(((bf16[27,32,128]{2,1,0:T(8,128)(2,1)}), bf16[27,256,128]{2,1,0:T(8,128)(2,1)}) %all-gather.3.cloned.1.call-update) | async-done | bytes 1769488 | tf_op jit(solution)/shard_map/all_gather | solution.py:115
  191.2 2.9 %copy.70 = bf16[27,256,128]{2,1,0:T(8,128)(2,1)} copy(bf16[27,256,128]{2,1,0:T(8,128)(2,1)} %all-gather.3.cloned.1.call-done) | data formatting | bytes 3538944
  (5 shorter events, 0.0 us)
Async XLA Ops:
  7.2 21.2 %copy-start = (bf16[128,16]{0,1:T(8,128)(2,1)S(1)}, bf16[128,16]{0,1:T(8,128)(2,1)}, u32[]{:S(2)}) copy-start(bf16[128,16]{0,1:T(8,128)(2,1)} %param.11) | copy-start | bytes 12292
  7.2 13.6 %copy-start.1 = (bf16[27,256,128]{2,1,0:T(8,128)(2,1)S(1)}, bf16[27,256,128]{2,1,0:T(8,128)(2,1)}, u32[]{:S(2)}) copy-start(bf16[27,256,128]{2,1,0:T(8,128)(2,1)} %param.10) | copy-start | bytes 5308420
  7.2 132.1 %reduce-scatter.2.cloned.1.call-start = ((), (), s32[]{:S(2)}) async-start(), calls=%async_computation.1 | async-start | bytes 3981312 | tf_op jit(solution)/shard_map/reduce_scatter | solution.py:90
  8.7 9.4 %collective-permute-start = (bf16[2,2,16,8,128]{4,0,3,2,1:T(2,128)(2,1)S(1)}, bf16[2,2,16,8,128]{4,0,3,2,1:T(2,128)(2,1)S(1)}, u32[]{:S(2)}, u32[]{:S(2)}) collective-permute-start(bf16[2,2,16,8,128]{4,0,3,2,1:T(2,128)(2,1)S(1)} %slice.51), channel_id=1, source_target_pairs={{0,2},{1,3},{4,6},{5,7},{8,10},{9,11},{12,14},{13,15},{16,18},{17,... | collective-permute-start | bytes 393224 | tf_op jit(solution)/shard_map/ppermute | solution.py:13
  20.8 6.5 %copy-start.3 = (bf16[2,6,16,8,256]{4,0,3,2,1:T(2,128)(2,1)}, bf16[2,6,16,8,256]{4,0,3,2,1:T(2,128)(2,1)S(1)}, u32[]{:S(2)}) copy-start(bf16[2,6,16,8,256]{4,0,3,2,1:T(2,128)(2,1)S(1)} %constant_dynamic-update-slice_fusion) | copy-start | bytes 2359300
  27.3 5.3 %copy-start.4 = (bf16[1,4,16,128]{3,2,1,0:T(8,128)(2,1)S(1)}, bf16[1,4,16,128]{3,2,1,0:T(8,128)(2,1)}, u32[]{:S(2)}) copy-start(bf16[1,4,16,128]{3,2,1,0:T(8,128)(2,1)} %param.15) | copy-start | bytes 49156
  59.0 132.2 %all-gather.3.cloned.1.call-start = ((), (), s32[]{:S(2)}) async-start(), calls=%async_computation.2 | async-start | bytes 1990656 | tf_op jit(solution)/shard_map/all_gather | solution.py:115
  146.9 17.6 %collective-permute-start.1 = (f32[2,2,16,8,256]{4,0,3,2,1:T(2,128)S(1)}, f32[2,2,16,8,256]{4,0,3,2,1:T(2,128)S(1)}, u32[]{:S(2)}, u32[]{:S(2)}) collective-permute-start(f32[2,2,16,8,256]{4,0,3,2,1:T(2,128)S(1)} %fusion.8), channel_id=1, source_target_pairs={{2,0},{3,1},{6,4},{7,5},{10,8},{11,9},{14,12},{15,13},{18,16},{19,... | collective-permute-start | bytes 1572872 | tf_op jit(solution)/shard_map/ppermute | solution.py:13
  153.1 12.4 %copy-start.2 = (bf16[2,4,16,8,128]{4,3,2,1,0:T(8,128)(2,1)S(1)}, bf16[2,4,16,8,128]{4,3,2,1,0:T(8,128)(2,1)}, u32[]{:S(2)}) copy-start(bf16[2,4,16,8,128]{4,3,2,1,0:T(8,128)(2,1)} %get-tuple-element.38) | copy-start | bytes 786436
  165.4 21.0 %collective-permute-start.2 = (bf16[2,4,16,8,128]{4,0,3,2,1:T(2,128)(2,1)S(1)}, bf16[2,4,16,8,128]{4,0,3,2,1:T(2,128)(2,1)S(1)}, u32[]{:S(2)}, u32[]{:S(2)}) collective-permute-start(bf16[2,4,16,8,128]{4,0,3,2,1:T(2,128)(2,1)S(1)} %constant_dynamic-slice_fusion), channel_id=1, source_target_pairs={{0,1},{1,0},{2,3},{3,2},{4,5},{5,4},{6,7},{7,6},{8,9},{9,8},{10,11... | collective-permute-start | bytes 786440 | tf_op jit(solution)/shard_map/ppermute | solution.py:113
Sparse Core Ops, SparseCore 0:
  59.1 80.1 reduce-scatter.1
  141.4 49.7 all-gather.2

commit v3 on v2

--- a/solution.py
+++ b/solution.py
@@ -11,6 +11,26 @@
     size = lax.axis_size(axis)
     pairs = [(i, i + by) for i in range(size) if 0 <= i + by < size]
     return lax.ppermute(shard, axis, pairs)
+
+
+def gathered(block, axis):
+    size = lax.axis_size(axis)
+    if size & (size - 1):
+        return lax.all_gather(block, axis, axis=0, tiled=True)
+    index = lax.axis_index(axis)
+    blocks = block
+    step = 1
+    while step < size:
+        pairs = [(i, i ^ step) for i in range(size)]
+        other = lax.ppermute(blocks, axis, pairs)
+        upper = (index & step) != 0
+        blocks = jnp.where(
+            upper,
+            jnp.concatenate([other, blocks], axis=0),
+            jnp.concatenate([blocks, other], axis=0),
+        )
+        step *= 2
+    return blocks
 
 
 def conv3d(lhs, rhs, padding, specs):
@@ -57,18 +77,17 @@
     latent = lax.psum(latent_part, "chan").astype(jnp.bfloat16)
     mixing = joining_matrix(rig_sizes, camera_order, owner_slot)
     cam_index = lax.axis_index("cam")
-    cam_count = lax.axis_size("cam")
     my_row = lax.dynamic_slice_in_dim(mixing, cam_index, 1, 0)
     latent_maps = latent.reshape(cam_dev, frames, height, width * lat_width)
-    both = jnp.concatenate([latent_maps, cotangent], axis=0)
-    both_in = lax.all_gather(both, "cam", axis=0, tiled=False)
-    flat_in = both_in[:, :cam_dev].reshape(cam_count * cam_dev, -1).astype(jnp.float32)
+    block_in = gathered(latent_maps, "cam")
+    flat_in = block_in.reshape(block_in.shape[0], -1).astype(jnp.float32)
     added = jnp.dot(
         my_row, flat_in, precision=lax.Precision.HIGHEST, preferred_element_type=jnp.float32
     )
     robot_latent = added.reshape(1, frames, height, width * lat_width)
     my_cols = lax.dynamic_slice_in_dim(mixing, cam_index * cam_dev, cam_dev, 1)
-    flat_in = both_in[:, cam_dev:].reshape(cam_count * cotangent.shape[0], -1).astype(jnp.float32)
+    block_in = gathered(cotangent, "cam")
+    flat_in = block_in.reshape(block_in.shape[0], -1).astype(jnp.float32)
     spread = lax.dot_general(
         my_cols,
         flat_in,
@@ -88,7 +107,7 @@
     grad_conv_local = conv3d(timed, dpre5, space_pad, ("CDHWN", "IDHWO", "DHWNC"))
     grad_conv_local = grad_conv_local.reshape(KT * KS * KS, -1, out_half)
     grad_conv_part = lax.psum_scatter(
-        grad_conv_local, ("cam", "tm"), scatter_dimension=1, tiled=True
+        grad_conv_local.astype(jnp.bfloat16), ("cam", "tm"), scatter_dimension=1, tiled=True
     )
     grad_proj = lax.psum(grad_proj_local, ("cam", "tm"))
     flipped = kernel[::-1, ::-1, ::-1]

time: 201 us -> 178 us (0.89)
  waiting for transfers between devices: 95.2 us -> 72.1 us
  blocking collectives: 41.5 us -> 34.5 us
  starting transfers between devices: 6.51 us -> 11.9 us
    reduce_scatter x1, waiting for transfers between devices: 80.1 us -> 54.7 us  [body(): lax.psum_scatter(grad_conv_local.astype(jnp.bfloat16), ('cam', 'tm'), sca...]
    all_gather x1 -> x0, blocking collectives: 14 us -> none  [body(): both_in = lax.all_gather(both, 'cam', axis=0, tiled=False)]
    ppermute x0 -> x4, waiting for transfers between devices: none -> 11.5 us  [gathered(): other = lax.ppermute(blocks, axis, pairs)]
    ppermute x2, waiting for transfers between devices: 11.3 us -> 0.01 us  [shifted(): return lax.ppermute(shard, axis, pairs)]
    psum x1, blocking collectives: 19.7 us -> 26.7 us  [body(): grad_proj = lax.psum(grad_proj_local, ('cam', 'tm'))]
    ppermute x0 -> x4, starting transfers between devices: none -> 6.84 us  [gathered(): other = lax.ppermute(blocks, axis, pairs)]
    all_gather x1, waiting for transfers between devices: 3.7 us -> 5.83 us  [body(): lax.all_gather(grad_conv_part.astype(jnp.bfloat16), ('cam', 'tm'), axis=1...]
    unnamed x14 -> x19, local copies, waits for them, and re-layouts: 5.17 us -> 6.06 us
  transfers between devices with their start and end apart: 5 -> 9, of which waited for: 3 -> 4; matrix products, arithmetic and copies ran while one was open for 8% -> 13% of each run, Pallas kernels for 0% -> 0%
where the time goes in v3:
time: 178 us
  waiting for transfers between devices  72.1 us (41%)
  blocking collectives  34.5 us (19%)
  matrix products  30 us (17%)
  between operations  14.3 us (8%)
  starting transfers between devices  11.9 us (7%)
  local copies, waits for them, and re-layouts  9.34 us (5%)
  other arithmetic  5.63 us (3%)
    reduce_scatter x1, waiting for transfers between devices, body(): lax.psum_scatter(grad_conv_local.astype(jnp.bfloat16), ('cam', 'tm'), sca...  54.7 us
    psum x1, blocking collectives, body(): grad_proj = lax.psum(grad_proj_local, ('cam', 'tm'))  26.7 us
    conv_general_dilated x4, matrix products, conv3d(): lax.conv_general_dilated(lhs, rhs, window_strides=(1, 1, 1), padding=padd...  26.5 us
    ppermute x4, waiting for transfers between devices, gathered(): other = lax.ppermute(blocks, axis, pairs)  11.5 us
    ppermute x4, starting transfers between devices, gathered(): other = lax.ppermute(blocks, axis, pairs)  6.84 us
    unnamed x19, local copies, waits for them, and re-layouts  6.06 us
    all_gather x1, waiting for transfers between devices, body(): lax.all_gather(grad_conv_part.astype(jnp.bfloat16), ('cam', 'tm'), axis=1...  5.83 us
    ppermute x2, starting transfers between devices, shifted(): return lax.ppermute(shard, axis, pairs)  4.69 us
  transfers between devices with their start and end apart: 9, of which 4 were waited for; matrix products, arithmetic and copies ran while one was open for 13% of the time, Pallas kernels for 0%

profile of v3, /device:TPU:0, one launch (start us, length us, event | category | flops | bytes accessed | tf_op | source)
XLA Modules:
  0.0 177.8 jit_solution(1386586239783750223)
XLA Ops:
  7.2 0.0 copy-start
  7.2 0.0 reduce-scatter.2.cloned.1.call-start
  7.2 3.1 %collective-permute-start.3 = (bf16[1,4,16,128]{3,2,1,0:T(8,128)(2,1)}, bf16[1,4,16,128]{3,2,1,0:T(8,128)(2,1)S(1)}, u32[]{:S(2)}, u32[]{:S(2)}) collective-permute-start(bf16[1,4,16,128]{3,2,1,0:T(8,128)(2,1)} %param.15), channel_id=1, source_target_pairs={{0,4},{4,0},{8,12},{12,8},{1,5},{5,1},{9,13},{13,9},{2,6},{6,2},{1... | collective-permute-start | bytes 49160 | tf_op jit(solution)/shard_map/ppermute | solution.py:25
  10.3 1.2 copy.37
  11.5 0.1 slice.43
  11.6 3.4 %collective-permute-start = (bf16[2,2,16,8,128]{4,0,3,2,1:T(2,128)(2,1)S(1)}, bf16[2,2,16,8,128]{4,0,3,2,1:T(2,128)(2,1)S(1)}, u32[]{:S(2)}, u32[]{:S(2)}) collective-permute-start(bf16[2,2,16,8,128]{4,0,3,2,1:T(2,128)(2,1)S(1)} %slice.43), channel_id=1, source_target_pairs={{0,2},{1,3},{4,6},{5,7},{8,10},{9,11},{12,14},{13,15},{16,18},{17,... | collective-permute-start | bytes 393224 | tf_op jit(solution)/shard_map/ppermute | solution.py:13
  15.0 0.8 reduce-window.8
  15.9 0.7 convert_reduce_fusion
  16.6 0.8 select_reduce_fusion.1
  17.4 0.0 copy-start.4
  17.4 2.2 %all_gather.10 = bf16[2,4,16,8,256]{4,0,3,2,1:T(2,128)(2,1)S(1)} all-gather(bf16[2,4,16,8,128]{4,0,3,2,1:T(2,128)(2,1)S(1)} %copy.37), channel_id=1, replica_groups=mesh['groups'=2,'cam'=4,'tm'=2,'chan'=2] {'chan'}, dimensions={4}, use_global_device_ids=true | all-gather | bytes 786432 | tf_op jit(solution)/shard_map/all_gather | solution.py:66
  19.6 0.9 copy.67
  20.5 0.0 collective-permute-done.3
  20.5 0.8 maximum_select_fusion.5
  21.3 2.6 %collective-permute-start.4 = (bf16[2,4,16,128]{3,2,1,0:T(8,128)(2,1)S(1)}, bf16[2,4,16,128]{3,2,1,0:T(8,128)(2,1)S(1)}, u32[]{:S(2)}, u32[]{:S(2)}) collective-permute-start(bf16[2,4,16,128]{3,2,1,0:T(8,128)(2,1)S(1)} %maximum_select_fusion.5), channel_id=1, source_target_pairs={{0,8},{4,12},{8,0},{12,4},{1,9},{5,13},{9,1},{13,5},{2,10},{6,14},... | collective-permute-start | bytes 98312 | tf_op jit(solution)/shard_map/ppermute | solution.py:25
  23.9 0.2 broadcast_select_fusion
  24.1 2.3 %collective-permute-done.4 = bf16[2,4,16,128]{3,2,1,0:T(8,128)(2,1)S(1)} collective-permute-done((bf16[2,4,16,128]{3,2,1,0:T(8,128)(2,1)S(1)}, bf16[2,4,16,128]{3,2,1,0:T(8,128)(2,1)S(1)}, u32[]{:S(2)}, u32[]{:S(2)}) %collective-permute-start.4) | collective-permute-done | bytes 32800 | tf_op jit(solution)/shard_map/ppermute | solution.py:25
  26.4 0.4 convolution_convert_fusion
  26.8 0.2 reshape.139
  27.0 0.0 collective-permute-done
  27.0 2.0 %all_gather.9 = bf16[2,2,16,8,256]{4,0,3,2,1:T(2,128)(2,1)S(1)} all-gather(bf16[2,2,16,8,128]{4,0,3,2,1:T(2,128)(2,1)S(1)} %collective-permute-done), channel_id=1, replica_groups=mesh['groups'=2,'cam'=4,'tm'=2,'chan'=2] {'chan'}, dimensions={4}, use_global_device_ids=true | all-gather | bytes 393216 | tf_op jit(solution)/shard_map/all_gather | solution.py:67
  29.0 0.2 constant_dynamic-update-slice_fusion.1
  29.2 0.4 constant_dynamic-update-slice_fusion
  29.7 0.0 copy-done.4
  29.7 6.6 %fusion.26 = f32[2,4,16,8,128]{4,0,3,2,1:T(2,128)S(1)} fusion(bf16[2,6,16,8,256]{4,0,3,2,1:T(2,128)(2,1)S(1)} %constant_dynamic-update-slice_fusion, bf16[3,3,3,256,128]{4,3,2,1,0:T(8,128)(2,1)S(1)} %bitcast.74), kind=kOutput, calls=%fused_computation.55 | convolution fusion | flops 1591738368 | bytes 3080192 | tf_op jit(solution)/shard_map/conv_general_dilated | solution.py:37
  36.3 0.2 multiply_convert_fusion
  36.4 0.9 fusion.5
  37.4 0.2 fusion.1
  37.6 10.0 %convolution_convert_fusion.1 = bf16[3,3,3,256,128]{4,3,2,1,0:T(8,128)(2,1)} fusion(bf16[2,6,16,8,256]{4,0,3,2,1:T(2,128)(2,1)S(1)} %constant_dynamic-update-slice_fusion, bf16[2,4,16,8,128]{4,3,2,1,0:T(8,128)(2,1)S(1)} %bitcast.79), kind=kOutput, calls=%fused_computation.1 | convolution fusion | flops 1592623104 | bytes 2818048 | tf_op jit(solution)/shard_map/conv_general_dilated | solution.py:37
  47.6 0.0 reduce-scatter.2.cloned.1.call-update
  47.6 0.2 all-gather.2.cloned.1.call-start
  47.8 1.4 rev.3
  49.3 0.3 copy.42
  49.6 0.0 copy-start.3
  49.6 4.9 %fusion.8 = f32[2,2,16,8,256]{4,0,3,2,1:T(2,128)} fusion(bf16[3,3,3,256,128]{4,3,2,1,0:T(8,128)(2,1)} %rev.3, bf16[2,4,16,8,128]{4,0,3,2,1:T(2,128)(2,1)S(1)} %copy.42), kind=kOutput, calls=%fused_computation.17 | convolution fusion | flops 397934592 | bytes 2424832 | tf_op jit(solution)/shard_map/conv_general_dilated | solution.py:37
  54.5 5.0 %fusion.23 = f32[2,4,16,8,256]{4,0,3,2,1:T(2,128)S(1)} fusion(bf16[3,3,3,256,128]{4,3,2,1,0:T(8,128)(2,1)S(1)} %bitcast.76, bf16[2,4,16,8,128]{4,3,2,1,0:T(8,128)(2,1)S(1)} %bitcast.81), kind=kOutput, calls=%fused_computation.52 | convolution fusion | flops 1193803776 | bytes 3080192 | tf_op jit(solution)/shard_map/conv_general_dilated | solution.py:37
  59.5 54.7 %reduce-scatter.2.cloned.1.call-done = bf16[27,32,128]{2,1,0:T(8,128)(2,1)} async-done(((bf16[27,256,128]{2,1,0:T(8,128)(2,1)}), bf16[27,32,128]{2,1,0:T(8,128)(2,1)}) %reduce-scatter.2.cloned.1.call-update) | async-done | bytes 221200 | tf_op jit(solution)/shard_map/reduce_scatter | solution.py:109
  114.2 0.0 all-gather.2.cloned.1.call-update
  114.2 1.1 fusion.27
  115.4 3.6 %psum.14 = bf16[1024,16]{0,1:T(8,128)(2,1)S(1)} all-reduce(f32[1024,16]{0,1:T(8,128)S(1)} %fusion.27), channel_id=1, replica_groups=mesh['groups'=2,'cam'=4,'tm'=2,'chan'=2] {'chan'}, use_global_device_ids=true, to_apply=%region_4.5 | all-reduce | flops 16384 | bytes 98304 | tf_op jit(solution)/shard_map/psum | solution.py:77
  119.0 0.2 copy.40
  119.2 0.2 reshape.137
  119.4 0.3 concatenate.62
  119.6 1.3 collective-permute-start.5
  120.9 1.1 collective-permute-start.1
  122.0 0.2 fusion.28
  122.2 26.7 %psum.15 = f32[128,16]{0,1:T(8,128)} all-reduce(f32[128,16]{0,1:T(8,128)S(1)} %fusion.28), channel_id=1, replica_groups=mesh['groups'=2,'cam'=4,'tm'=2,'chan'=2] {'cam','tm'}, use_global_device_ids=true, to_apply=%region_6.7 | all-reduce | flops 2048 | bytes 16384 | tf_op jit(solution)/shard_map/psum | solution.py:112
  148.9 0.0 collective-permute-done.1
  148.9 0.1 collective-permute-start.2
  149.1 0.1 maximum_select_fusion.2
  149.2 9.2 %collective-permute-done.2 = bf16[4,4,16,128]{3,2,1,0:T(8,128)(2,1)S(1)} collective-permute-done((bf16[4,4,16,128]{3,2,1,0:T(8,128)(2,1)S(1)}, bf16[4,4,16,128]{3,2,1,0:T(8,128)(2,1)S(1)}, u32[]{:S(2)}, u32[]{:S(2)}) %collective-permute-start.2) | collective-permute-done | bytes 65568 | tf_op jit(solution)/shard_map/ppermute | solution.py:25
  158.4 0.1 copy.66
  158.5 0.0 collective-permute-done.5
  158.5 0.3 fusion.2
  158.8 0.4 convert_element_type.57
  159.2 0.2 constant_dynamic-slice_fusion
  159.4 0.1 collective-permute-start.6
  159.5 0.1 maximum_select_fusion
  159.6 1.6 fusion.20
  161.2 0.0 collective-permute-done.6
  161.2 0.3 add_convert_fusion
  161.5 0.7 copy.47
  162.2 5.8 %all-gather.2.cloned.1.call-done = bf16[27,256,128]{2,1,0:T(8,128)(2,1)} async-done(((bf16[27,32,128]{2,1,0:T(8,128)(2,1)}), bf16[27,256,128]{2,1,0:T(8,128)(2,1)}) %all-gather.2.cloned.1.call-update) | async-done | bytes 1769488 | tf_op jit(solution)/shard_map/all_gather | solution.py:134
  168.0 2.9 %copy.74 = bf16[27,256,128]{2,1,0:T(8,128)(2,1)} copy(bf16[27,256,128]{2,1,0:T(8,128)(2,1)} %all-gather.2.cloned.1.call-done) | data formatting | bytes 3538944
  (12 shorter events, 0.1 us)
Async XLA Ops:
  7.2 30.2 %copy-start = (bf16[128,16]{0,1:T(8,128)(2,1)S(1)}, bf16[128,16]{0,1:T(8,128)(2,1)}, u32[]{:S(2)}) copy-start(bf16[128,16]{0,1:T(8,128)(2,1)} %param.11) | copy-start | bytes 12292
  7.2 107.0 %reduce-scatter.2.cloned.1.call-start = ((), (), s32[]{:S(2)}) async-start(), calls=%async_computation.1 | async-start | bytes 1990656 | tf_op jit(solution)/shard_map/reduce_scatter | solution.py:109
  7.2 13.2 %collective-permute-start.3 = (bf16[1,4,16,128]{3,2,1,0:T(8,128)(2,1)}, bf16[1,4,16,128]{3,2,1,0:T(8,128)(2,1)S(1)}, u32[]{:S(2)}, u32[]{:S(2)}) collective-permute-start(bf16[1,4,16,128]{3,2,1,0:T(8,128)(2,1)} %param.15), channel_id=1, source_target_pairs={{0,4},{4,0},{8,12},{12,8},{1,5},{5,1},{9,13},{13,9},{2,6},{6,2},{1... | collective-permute-start | bytes 49160 | tf_op jit(solution)/shard_map/ppermute | solution.py:25
  11.6 15.4 %collective-permute-start = (bf16[2,2,16,8,128]{4,0,3,2,1:T(2,128)(2,1)S(1)}, bf16[2,2,16,8,128]{4,0,3,2,1:T(2,128)(2,1)S(1)}, u32[]{:S(2)}, u32[]{:S(2)}) collective-permute-start(bf16[2,2,16,8,128]{4,0,3,2,1:T(2,128)(2,1)S(1)} %slice.43), channel_id=1, source_target_pairs={{0,2},{1,3},{4,6},{5,7},{8,10},{9,11},{12,14},{13,15},{16,18},{17,... | collective-permute-start | bytes 393224 | tf_op jit(solution)/shard_map/ppermute | solution.py:13
  17.4 12.3 %copy-start.4 = (f32[4,8]{1,0:T(4,128)}, f32[4,8]{1,0:T(4,128)S(1)}, u32[]{:S(2)}) copy-start(f32[4,8]{1,0:T(4,128)S(1)} %fusion.17) | copy-start | bytes 388
  19.6 10.1 %copy-start.1 = (bf16[27,256,128]{2,1,0:T(8,128)(2,1)S(1)}, bf16[27,256,128]{2,1,0:T(8,128)(2,1)}, u32[]{:S(2)}) copy-start(bf16[27,256,128]{2,1,0:T(8,128)(2,1)} %param.10) | copy-start | bytes 5308420
  21.3 5.1 %collective-permute-start.4 = (bf16[2,4,16,128]{3,2,1,0:T(8,128)(2,1)S(1)}, bf16[2,4,16,128]{3,2,1,0:T(8,128)(2,1)S(1)}, u32[]{:S(2)}, u32[]{:S(2)}) collective-permute-start(bf16[2,4,16,128]{3,2,1,0:T(8,128)(2,1)S(1)} %maximum_select_fusion.5), channel_id=1, source_target_pairs={{0,8},{4,12},{8,0},{12,4},{1,9},{5,13},{9,1},{13,5},{2,10},{6,14},... | collective-permute-start | bytes 98312 | tf_op jit(solution)/shard_map/ppermute | solution.py:25
  37.6 11.7 %copy-start.2 = (bf16[1024,128]{1,0:T(8,128)(2,1)}, bf16[1024,128]{1,0:T(8,128)(2,1)S(1)}, u32[]{:S(2)}) copy-start(bf16[1024,128]{1,0:T(8,128)(2,1)S(1)} %fusion.1) | copy-start | bytes 786436
  47.6 120.4 %all-gather.2.cloned.1.call-start = ((), (), s32[]{:S(2)}) async-start(), calls=%async_computation.2 | async-start | bytes 1990656 | tf_op jit(solution)/shard_map/all_gather | solution.py:134
  49.6 5.0 %copy-start.3 = (bf16[1024,128]{1,0:T(8,128)(2,1)S(1)}, bf16[1024,128]{1,0:T(8,128)(2,1)}, u32[]{:S(2)}) copy-start(bf16[1024,128]{1,0:T(8,128)(2,1)} %copy-done.2) | copy-start | bytes 786436
  119.6 38.8 %collective-permute-start.5 = (f32[2,2,16,8,256]{4,0,3,2,1:T(2,128)}, f32[2,2,16,8,256]{4,0,3,2,1:T(2,128)S(1)}, u32[]{:S(2)}, u32[]{:S(2)}) collective-permute-start(f32[2,2,16,8,256]{4,0,3,2,1:T(2,128)} %fusion.8), channel_id=1, source_target_pairs={{2,0},{3,1},{6,4},{7,5},{10,8},{11,9},{14,12},{15,13},{18,16},{19,... | collective-permute-start | bytes 1572872 | tf_op jit(solution)/shard_map/ppermute | solution.py:13
  120.9 28.0 %collective-permute-start.1 = (bf16[2,4,16,128]{3,2,1,0:T(8,128)(2,1)S(1)}, bf16[2,4,16,128]{3,2,1,0:T(8,128)(2,1)S(1)}, u32[]{:S(2)}, u32[]{:S(2)}) collective-permute-start(bf16[2,4,16,128]{3,2,1,0:T(8,128)(2,1)S(1)} %reshape.137), channel_id=1, source_target_pairs={{0,4},{4,0},{8,12},{12,8},{1,5},{5,1},{9,13},{13,9},{2,6},{6,2},{1... | collective-permute-start | bytes 98312 | tf_op jit(solution)/shard_map/ppermute | solution.py:25
  148.9 9.5 %collective-permute-start.2 = (bf16[4,4,16,128]{3,2,1,0:T(8,128)(2,1)S(1)}, bf16[4,4,16,128]{3,2,1,0:T(8,128)(2,1)S(1)}, u32[]{:S(2)}, u32[]{:S(2)}) collective-permute-start(bf16[4,4,16,128]{3,2,1,0:T(8,128)(2,1)S(1)} %maximum_select_fusion.1), channel_id=1, source_target_pairs={{0,8},{4,12},{8,0},{12,4},{1,9},{5,13},{9,1},{13,5},{2,10},{6,14},... | collective-permute-start | bytes 196616 | tf_op jit(solution)/shard_map/ppermute | solution.py:25
  159.4 1.8 collective-permute-start.6
Sparse Core Ops, SparseCore 0:
  47.7 66.4 reduce-scatter.1
  116.5 51.5 all-gather.1

commit v4 on v3

--- a/solution.py
+++ b/solution.py
@@ -11,6 +11,53 @@
     size = lax.axis_size(axis)
     pairs = [(i, i + by) for i in range(size) if 0 <= i + by < size]
     return lax.ppermute(shard, axis, pairs)
+
+
+def group_place(axes):
+    count = 1
+    index = 0
+    for axis in axes:
+        count *= lax.axis_size(axis)
+        index = index * lax.axis_size(axis) + lax.axis_index(axis)
+    return count, index
+
+
+def from_all(block, axes, count):
+    received = [block]
+    for step in range(1, count):
+        pairs = [(i, (i - step) % count) for i in range(count)]
+        received.append(lax.ppermute(block, axes, pairs))
+    return jnp.stack(received, 0)
+
+
+def rows_scatter_sum(rows, axes):
+    count, index = group_place(axes)
+    if count > 8:
+        return lax.psum_scatter(rows, axes, scatter_dimension=0, tiled=True)
+    piece = rows.shape[0] // count
+    summed = lax.dynamic_slice_in_dim(rows, index * piece, piece, 0)
+    for step in range(1, count):
+        target = (index + step) % count
+        part = lax.dynamic_slice_in_dim(rows, target * piece, piece, 0)
+        pairs = [(i, (i + step) % count) for i in range(count)]
+        summed = summed + lax.ppermute(part, axes, pairs)
+    return summed
+
+
+def rows_gather(rows, axes):
+    count, index = group_place(axes)
+    if count > 8:
+        return lax.all_gather(rows, axes, axis=0, tiled=True)
+    stacked = jnp.roll(from_all(rows, axes, count), index, axis=0)
+    return stacked.reshape(count * rows.shape[0], *rows.shape[1:])
+
+
+def ordered_sum(block, axes):
+    count, index = group_place(axes)
+    if count > 8:
+        return lax.psum(block, axes)
+    stacked = jnp.roll(from_all(block, axes, count), index, axis=0)
+    return jnp.sum(stacked, axis=0)
 
 
 def gathered(block, axis):
@@ -105,11 +152,9 @@
     dpre = (dact * sigma * (1.0 + pre * (1.0 - sigma))).astype(jnp.bfloat16)
     dpre5 = dpre.reshape(cam_dev, frames, height, width, out_half)
     grad_conv_local = conv3d(timed, dpre5, space_pad, ("CDHWN", "IDHWO", "DHWNC"))
-    grad_conv_local = grad_conv_local.reshape(KT * KS * KS, -1, out_half)
-    grad_conv_part = lax.psum_scatter(
-        grad_conv_local.astype(jnp.bfloat16), ("cam", "tm"), scatter_dimension=1, tiled=True
-    )
-    grad_proj = lax.psum(grad_proj_local, ("cam", "tm"))
+    grad_conv_rows = grad_conv_local.reshape(-1, out_half)
+    grad_conv_part = rows_scatter_sum(grad_conv_rows, ("cam", "tm"))
+    grad_proj = ordered_sum(grad_proj_local, ("cam", "tm"))
     flipped = kernel[::-1, ::-1, ::-1]
     back_specs = ("NDHWC", "DHWOI", "NDHWC")
     head_pad = [(KT - 1, 0), (pad_half, pad_half), (pad_half, pad_half)]
@@ -131,8 +176,8 @@
         pairs = [(i, (i + step) % chan_count) for i in range(chan_count)]
         summed = summed + lax.ppermute(sent, "chan", pairs).astype(jnp.float32)
     grad_video = summed.astype(jnp.bfloat16)
-    grad_conv = lax.all_gather(
-        grad_conv_part.astype(jnp.bfloat16), ("cam", "tm"), axis=1, tiled=True
+    grad_conv = rows_gather(grad_conv_part.astype(jnp.bfloat16), ("cam", "tm")).reshape(
+        KT * KS * KS, -1, out_half
     )
     return (robot_latent, grad_conv, grad_proj, grad_video)
 

time: 178 us -> 222 us (1.25)
  the two profiles are of different devices: /device:TPU:0 before, /device:TPU:7 now
where the time goes in v4:
time: 222 us; the launch traced here: 221 us
  waiting for transfers between devices  73.7 us (33%)
  starting transfers between devices  65.4 us (29%)
  local copies, waits for them, and re-layouts  31.9 us (14%)
  matrix products  29.1 us (13%)
  blocking collectives  12.2 us (5%)
  other arithmetic  7.42 us (3%)
    ppermute x14, waiting for transfers between devices, from_all(): received.append(lax.ppermute(block, axes, pairs))  42.4 us
    ppermute x14, starting transfers between devices, from_all(): received.append(lax.ppermute(block, axes, pairs))  29.2 us
    ppermute x7, starting transfers between devices, rows_scatter_sum(): summed = summed + lax.ppermute(part, axes, pairs)  27 us
    conv_general_dilated x4, matrix products, conv3d(): lax.conv_general_dilated(lhs, rhs, window_strides=(1, 1, 1), padding=padd...  25.3 us
    unnamed x48, local copies, waits for them, and re-layouts  18.2 us
    ppermute x7, waiting for transfers between devices, rows_scatter_sum(): summed = summed + lax.ppermute(part, axes, pairs)  17.3 us
    ppermute x4, waiting for transfers between devices, gathered(): other = lax.ppermute(blocks, axis, pairs)  14 us
    psum x1, blocking collectives, body(): latent = lax.psum(latent_part, 'chan').astype(jnp.bfloat16)  6.3 us
  transfers between devices with their start and end apart: 28, of which 8 were waited for; matrix products, arithmetic and copies ran while one was open for 27% of the time, Pallas kernels for 0%

profile of v4, /device:TPU:7, one launch (start us, length us, event | category | flops | bytes accessed | tf_op | source)
XLA Modules:
  0.0 220.8 jit_solution(12309530886719177653)
XLA Ops:
  0.7 1.4 collective-permute-start.3
  2.0 1.2 copy.37
  3.3 1.3 collective-permute-start
  4.6 0.8 reduce-window.8
  5.5 0.7 convert_reduce_fusion
  6.2 0.8 select_reduce_fusion.1
  7.0 2.8 %all_gather.7 = bf16[2,4,16,8,256]{4,0,3,2,1:T(2,128)(2,1)S(1)} all-gather(bf16[2,4,16,8,128]{4,0,3,2,1:T(2,128)(2,1)S(1)} %copy.37), channel_id=1, replica_groups=mesh['groups'=2,'cam'=4,'tm'=2,'chan'=2] {'chan'}, dimensions={4}, use_global_device_ids=true | all-gather | bytes 786432 | tf_op jit(solution)/shard_map/all_gather | solution.py:113
  9.8 0.9 copy.67
  10.7 2.9 %rev.3 = bf16[3,3,3,256,128]{4,3,2,1,0:T(8,128)(2,1)} reverse(bf16[3,3,3,256,128]{4,3,2,1,0:T(8,128)(2,1)} %bitcast.125), dimensions={0,1,2} | reverse | bytes 3538944 | tf_op jit(solution)/shard_map/rev | solution.py:158
  13.6 2.4 %collective-permute-start.4 = (bf16[2,4,16,128]{3,2,1,0:T(8,128)(2,1)S(1)}, bf16[2,4,16,128]{3,2,1,0:T(8,128)(2,1)S(1)}, u32[]{:S(2)}, u32[]{:S(2)}) collective-permute-start(bf16[2,4,16,128]{3,2,1,0:T(8,128)(2,1)S(1)} %maximum_select_fusion.5), channel_id=1, source_target_pairs={{0,8},{4,12},{8,0},{12,4},{1,9},{5,13},{9,1},{13,5},{2,10},{6,14},... | collective-permute-start | bytes 98312 | tf_op jit(solution)/shard_map/ppermute | solution.py:72
  16.2 1.4 collective-permute-done.4
  18.3 3.1 %all_gather.6 = bf16[2,2,16,8,256]{4,0,3,2,1:T(2,128)(2,1)S(1)} all-gather(bf16[2,2,16,8,128]{4,0,3,2,1:T(2,128)(2,1)S(1)} %collective-permute-done), channel_id=1, replica_groups=mesh['groups'=2,'cam'=4,'tm'=2,'chan'=2] {'chan'}, dimensions={4}, use_global_device_ids=true | all-gather | bytes 393216 | tf_op jit(solution)/shard_map/all_gather | solution.py:114
  22.1 6.6 %fusion.25 = f32[2,4,16,8,128]{4,0,3,2,1:T(2,128)S(1)} fusion(bf16[2,6,16,8,256]{4,0,3,2,1:T(2,128)(2,1)S(1)} %constant_dynamic-update-slice_fusion, bf16[3,3,3,256,128]{4,3,2,1,0:T(8,128)(2,1)S(1)} %bitcast.126), kind=kOutput, calls=%fused_computation.96 | convolution fusion | flops 1591738368 | bytes 3080192 | tf_op jit(solution)/shard_map/conv_general_dilated | solution.py:84
  28.9 0.8 constant_dynamic-update-slice_fusion.17
  29.7 2.0 collective-permute-start.25
  31.7 2.4 %collective-permute-start.24 = (f32[128,16]{0,1:T(8,128)S(1)}, f32[128,16]{0,1:T(8,128)}, u32[]{:S(2)}, u32[]{:S(2)}) collective-permute-start(f32[128,16]{0,1:T(8,128)S(1)} %get-tuple-element.49), channel_id=1, source_target_pairs={{0,4},{2,6},{4,8},{6,10},{8,12},{10,14},{12,0},{14,2},{1,5},{3,7},... | collective-permute-start | bytes 24584 | tf_op jit(solution)/shard_map/ppermute | solution.py:29
  34.4 1.0 collective-permute-start.22
  35.3 1.2 collective-permute-start.19
  37.2 6.0 %fusion.21 = f32[2,4,16,8,256]{4,0,3,2,1:T(2,128)} fusion(bf16[3,3,3,256,128]{4,3,2,1,0:T(8,128)(2,1)S(1)} %bitcast.127, bf16[2,4,16,8,128]{4,3,2,1,0:T(8,128)(2,1)S(1)} %bitcast.131), kind=kOutput, calls=%fused_computation.92 | convolution fusion | flops 1193803776 | bytes 3080192 | tf_op jit(solution)/shard_map/conv_general_dilated | solution.py:84
  43.2 9.2 %fusion.23 = f32[3,3,3,256,128]{4,3,2,1,0:T(8,128)S(1)} fusion(bf16[2,6,16,8,256]{4,0,3,2,1:T(2,128)(2,1)S(1)} %constant_dynamic-update-slice_fusion, bf16[2,4,16,8,128]{4,3,2,1,0:T(8,128)(2,1)S(1)} %bitcast.132), kind=kOutput, calls=%fused_computation.94 | convolution fusion | flops 1591738368 | bytes 4587520 | tf_op jit(solution)/shard_map/conv_general_dilated | solution.py:84
  52.4 0.8 fusion.26
  53.2 3.5 %fusion.8 = f32[2,2,16,8,256]{4,0,3,2,1:T(2,128)} fusion(bf16[3,3,3,256,128]{4,3,2,1,0:T(8,128)(2,1)S(1)} %copy-done.3, bf16[2,4,16,8,128]{4,0,3,2,1:T(2,128)(2,1)S(1)} %copy.42), kind=kOutput, calls=%fused_computation.33 | convolution fusion | flops 397934592 | bytes 2424832 | tf_op jit(solution)/shard_map/conv_general_dilated | solution.py:84
  56.7 1.7 constant_dynamic-slice_fusion.8
  58.4 6.3 %psum.7 = bf16[1024,16]{0,1:T(8,128)(2,1)} all-reduce(f32[1024,16]{0,1:T(8,128)} %fusion.26), channel_id=1, replica_groups=mesh['groups'=2,'cam'=4,'tm'=2,'chan'=2] {'chan'}, use_global_device_ids=true, to_apply=%region_4.5 | all-reduce | flops 16384 | bytes 98304 | tf_op jit(solution)/shard_map/psum | solution.py:124
  64.7 1.6 copy.40
  66.3 1.8 reshape.138
  68.1 1.8 concatenate.72
  69.9 2.4 %collective-permute-start.20 = (f32[128,16]{0,1:T(8,128)S(1)}, f32[128,16]{0,1:T(8,128)S(1)}, u32[]{:S(2)}, u32[]{:S(2)}) collective-permute-start(f32[128,16]{0,1:T(8,128)S(1)} %get-tuple-element.49), channel_id=1, source_target_pairs={{0,12},{2,14},{4,0},{6,2},{8,4},{10,6},{12,8},{14,10},{1,13},{3,15... | collective-permute-start | bytes 24584 | tf_op jit(solution)/shard_map/ppermute | solution.py:29
  72.4 1.3 constant_dynamic-update-slice_fusion.16
  73.7 2.7 %collective-permute-start.21 = (f32[128,16]{0,1:T(8,128)S(1)}, f32[128,16]{0,1:T(8,128)S(1)}, u32[]{:S(2)}, u32[]{:S(2)}) collective-permute-start(f32[128,16]{0,1:T(8,128)S(1)} %get-tuple-element.49), channel_id=1, source_target_pairs={{0,10},{2,12},{4,14},{6,0},{8,2},{10,4},{12,6},{14,8},{1,11},{3,13... | collective-permute-start | bytes 24584 | tf_op jit(solution)/shard_map/ppermute | solution.py:29
  76.9 1.0 collective-permute-done.21
  78.0 1.2 collective-permute-start.1
  79.8 1.3 constant_dynamic-update-slice_fusion.13
  81.1 1.5 collective-permute-start.11
  82.5 1.3 constant_dynamic-update-slice_fusion.12
  83.8 1.8 collective-permute-start.10
  85.6 1.3 constant_dynamic-update-slice_fusion.11
  86.9 2.9 %collective-permute-start.9 = (f32[864,128]{1,0:T(8,128)}, f32[864,128]{1,0:T(8,128)S(1)}, u32[]{:S(2)}, u32[]{:S(2)}) collective-permute-start(f32[864,128]{1,0:T(8,128)} %get-tuple-element.39), channel_id=1, source_target_pairs={{0,10},{2,12},{4,14},{6,0},{8,2},{10,4},{12,6},{14,8},{1,11},{3,13... | collective-permute-start | bytes 1327112 | tf_op jit(solution)/shard_map/ppermute | solution.py:43
  89.8 1.3 constant_dynamic-update-slice_fusion.10
  91.7 1.3 constant_dynamic-update-slice_fusion.8
  93.0 0.6 constant_dynamic-update-slice_fusion.7
  94.2 1.3 constant_dynamic-update-slice_fusion.5
  95.5 1.3 constant_dynamic-update-slice_fusion.4
  96.8 1.3 constant_dynamic-update-slice_fusion.3
  98.1 1.3 constant_dynamic-update-slice_fusion.2
  99.4 1.4 dynamic-slice_reduce_fusion
  100.9 0.8 maximum_select_fusion.1
  101.9 1.0 maximum_select_fusion.2
  102.9 12.6 %collective-permute-done.2 = bf16[4,4,16,128]{3,2,1,0:T(8,128)(2,1)S(1)} collective-permute-done((bf16[4,4,16,128]{3,2,1,0:T(8,128)(2,1)S(1)}, bf16[4,4,16,128]{3,2,1,0:T(8,128)(2,1)S(1)}, u32[]{:S(2)}, u32[]{:S(2)}) %collective-permute-start.2) | collective-permute-done | bytes 65568 | tf_op jit(solution)/shard_map/ppermute | solution.py:72
  115.5 11.5 %collective-permute-start.7 = (f32[864,128]{1,0:T(8,128)}, f32[864,128]{1,0:T(8,128)S(1)}, u32[]{:S(2)}, u32[]{:S(2)}) collective-permute-start(f32[864,128]{1,0:T(8,128)} %get-tuple-element.41), channel_id=1, source_target_pairs={{0,6},{2,8},{4,10},{6,12},{8,14},{10,0},{12,2},{14,4},{1,7},{3,9},... | collective-permute-start | bytes 1327112 | tf_op jit(solution)/shard_map/ppermute | solution.py:43
  127.0 9.3 %collective-permute-start.6 = (f32[864,128]{1,0:T(8,128)}, f32[864,128]{1,0:T(8,128)S(1)}, u32[]{:S(2)}, u32[]{:S(2)}) collective-permute-start(f32[864,128]{1,0:T(8,128)} %get-tuple-element.42), channel_id=1, source_target_pairs={{0,4},{2,6},{4,8},{6,10},{8,12},{10,14},{12,0},{14,2},{1,5},{3,7},... | collective-permute-start | bytes 1327112 | tf_op jit(solution)/shard_map/ppermute | solution.py:43
  136.5 2.3 %collective-permute-start.26 = (f32[2,2,16,8,256]{4,0,3,2,1:T(2,128)}, f32[2,2,16,8,256]{4,0,3,2,1:T(2,128)S(1)}, u32[]{:S(2)}, u32[]{:S(2)}) collective-permute-start(f32[2,2,16,8,256]{4,0,3,2,1:T(2,128)} %fusion.8), channel_id=1, source_target_pairs={{2,0},{3,1},{6,4},{7,5},{10,8},{11,9},{14,12},{15,13},{18,16},{19,... | collective-permute-start | bytes 1572872 | tf_op jit(solution)/shard_map/ppermute | solution.py:13
  138.8 1.6 fusion.18
  140.3 15.3 %collective-permute-done.7 = f32[864,128]{1,0:T(8,128)S(1)} collective-permute-done((f32[864,128]{1,0:T(8,128)}, f32[864,128]{1,0:T(8,128)S(1)}, u32[]{:S(2)}, u32[]{:S(2)}) %collective-permute-start.7) | collective-permute-done | bytes 442400 | tf_op jit(solution)/shard_map/ppermute | solution.py:43
  155.6 1.9 collective-permute-done.6
  157.7 9.2 %collective-permute-start.18 = (bf16[864,128]{1,0:T(8,128)(2,1)S(1)}, bf16[864,128]{1,0:T(8,128)(2,1)S(1)}, u32[]{:S(2)}, u32[]{:S(2)}) collective-permute-start(bf16[864,128]{1,0:T(8,128)(2,1)S(1)} %get-tuple-element.35), channel_id=1, source_target_pairs={{0,2},{2,4},{4,6},{6,8},{8,10},{10,12},{12,14},{14,0},{1,3},{3,5},... | collective-permute-start | bytes 663560 | tf_op jit(solution)/shard_map/ppermute | solution.py:29
  166.9 2.1 collective-permute-start.17
  169.4 2.2 %collective-permute-start.12 = (bf16[864,128]{1,0:T(8,128)(2,1)S(1)}, bf16[864,128]{1,0:T(8,128)(2,1)S(1)}, u32[]{:S(2)}, u32[]{:S(2)}) collective-permute-start(bf16[864,128]{1,0:T(8,128)(2,1)S(1)} %get-tuple-element.35), channel_id=1, source_target_pairs={{0,14},{2,0},{4,2},{6,4},{8,6},{10,8},{12,10},{14,12},{1,15},{3,1}... | collective-permute-start | bytes 663560 | tf_op jit(solution)/shard_map/ppermute | solution.py:29
  172.6 13.1 %collective-permute-done.12 = bf16[864,128]{1,0:T(8,128)(2,1)S(1)} collective-permute-done((bf16[864,128]{1,0:T(8,128)(2,1)S(1)}, bf16[864,128]{1,0:T(8,128)(2,1)S(1)}, u32[]{:S(2)}, u32[]{:S(2)}) %collective-permute-start.12) | collective-permute-done | bytes 221216 | tf_op jit(solution)/shard_map/ppermute | solution.py:29
  185.7 3.4 %collective-permute-start.13 = (bf16[864,128]{1,0:T(8,128)(2,1)S(1)}, bf16[864,128]{1,0:T(8,128)(2,1)S(1)}, u32[]{:S(2)}, u32[]{:S(2)}) collective-permute-start(bf16[864,128]{1,0:T(8,128)(2,1)S(1)} %get-tuple-element.35), channel_id=1, source_target_pairs={{0,12},{2,14},{4,0},{6,2},{8,4},{10,6},{12,8},{14,10},{1,13},{3,15... | collective-permute-start | bytes 663560 | tf_op jit(solution)/shard_map/ppermute | solution.py:29
  189.1 14.4 %collective-permute-done.13 = bf16[864,128]{1,0:T(8,128)(2,1)S(1)} collective-permute-done((bf16[864,128]{1,0:T(8,128)(2,1)S(1)}, bf16[864,128]{1,0:T(8,128)(2,1)S(1)}, u32[]{:S(2)}, u32[]{:S(2)}) %collective-permute-start.13) | collective-permute-done | bytes 221216 | tf_op jit(solution)/shard_map/ppermute | solution.py:29
  203.5 13.8 %collective-permute-done.14 = bf16[864,128]{1,0:T(8,128)(2,1)S(1)} collective-permute-done((bf16[864,128]{1,0:T(8,128)(2,1)S(1)}, bf16[864,128]{1,0:T(8,128)(2,1)S(1)}, u32[]{:S(2)}, u32[]{:S(2)}) %collective-permute-start.14) | collective-permute-done | bytes 221216 | tf_op jit(solution)/shard_map/ppermute | solution.py:29
  218.4 1.3 constant_dynamic-slice_fusion.1
  220.0 0.7 copy.47
  (82 shorter events, 8.3 us)
Async XLA Ops:
  0.6 36.1 %copy-start = (bf16[128,16]{0,1:T(8,128)(2,1)S(1)}, bf16[128,16]{0,1:T(8,128)(2,1)}, u32[]{:S(2)}) copy-start(bf16[128,16]{0,1:T(8,128)(2,1)} %param.11) | copy-start | bytes 12292
  0.6 13.0 %copy-start.4 = (bf16[1,4,16,128]{3,2,1,0:T(8,128)(2,1)S(1)}, bf16[1,4,16,128]{3,2,1,0:T(8,128)(2,1)}, u32[]{:S(2)}) copy-start(bf16[1,4,16,128]{3,2,1,0:T(8,128)(2,1)} %param.15) | copy-start | bytes 49156
  0.7 12.9 %collective-permute-start.3 = (bf16[1,4,16,128]{3,2,1,0:T(8,128)(2,1)}, bf16[1,4,16,128]{3,2,1,0:T(8,128)(2,1)S(1)}, u32[]{:S(2)}, u32[]{:S(2)}) collective-permute-start(bf16[1,4,16,128]{3,2,1,0:T(8,128)(2,1)} %param.15), channel_id=1, source_target_pairs={{0,4},{4,0},{8,12},{12,8},{1,5},{5,1},{9,13},{13,9},{2,6},{6,2},{1... | collective-permute-start | bytes 49160 | tf_op jit(solution)/shard_map/ppermute | solution.py:72
  3.3 14.9 %collective-permute-start = (bf16[2,2,16,8,128]{4,0,3,2,1:T(2,128)(2,1)S(1)}, bf16[2,2,16,8,128]{4,0,3,2,1:T(2,128)(2,1)S(1)}, u32[]{:S(2)}, u32[]{:S(2)}) collective-permute-start(bf16[2,2,16,8,128]{4,0,3,2,1:T(2,128)(2,1)S(1)} %slice.43), channel_id=1, source_target_pairs={{0,2},{1,3},{4,6},{5,7},{8,10},{9,11},{12,14},{13,15},{16,18},{17,... | collective-permute-start | bytes 393224 | tf_op jit(solution)/shard_map/ppermute | solution.py:13
  7.0 15.1 %copy-start.5 = (f32[4,8]{1,0:T(4,128)}, f32[4,8]{1,0:T(4,128)S(1)}, u32[]{:S(2)}) copy-start(f32[4,8]{1,0:T(4,128)S(1)} %fusion.16) | copy-start | bytes 388
  9.8 12.3 %copy-start.2 = (bf16[27,256,128]{2,1,0:T(8,128)(2,1)S(1)}, bf16[27,256,128]{2,1,0:T(8,128)(2,1)}, u32[]{:S(2)}) copy-start(bf16[27,256,128]{2,1,0:T(8,128)(2,1)} %param.10) | copy-start | bytes 5308420
  13.6 4.0 %collective-permute-start.4 = (bf16[2,4,16,128]{3,2,1,0:T(8,128)(2,1)S(1)}, bf16[2,4,16,128]{3,2,1,0:T(8,128)(2,1)S(1)}, u32[]{:S(2)}, u32[]{:S(2)}) collective-permute-start(bf16[2,4,16,128]{3,2,1,0:T(8,128)(2,1)S(1)} %maximum_select_fusion.5), channel_id=1, source_target_pairs={{0,8},{4,12},{8,0},{12,4},{1,9},{5,13},{9,1},{13,5},{2,10},{6,14},... | collective-permute-start | bytes 98312 | tf_op jit(solution)/shard_map/ppermute | solution.py:72
  29.7 57.2 %collective-permute-start.25 = (f32[128,16]{0,1:T(8,128)S(1)}, f32[128,16]{0,1:T(8,128)}, u32[]{:S(2)}, u32[]{:S(2)}) collective-permute-start(f32[128,16]{0,1:T(8,128)S(1)} %get-tuple-element.49), channel_id=1, source_target_pairs={{0,2},{2,4},{4,6},{6,8},{8,10},{10,12},{12,14},{14,0},{1,3},{3,5},... | collective-permute-start | bytes 24584 | tf_op jit(solution)/shard_map/ppermute | solution.py:29
  31.7 52.1 %collective-permute-start.24 = (f32[128,16]{0,1:T(8,128)S(1)}, f32[128,16]{0,1:T(8,128)}, u32[]{:S(2)}, u32[]{:S(2)}) collective-permute-start(f32[128,16]{0,1:T(8,128)S(1)} %get-tuple-element.49), channel_id=1, source_target_pairs={{0,4},{2,6},{4,8},{6,10},{8,12},{10,14},{12,0},{14,2},{1,5},{3,7},... | collective-permute-start | bytes 24584 | tf_op jit(solution)/shard_map/ppermute | solution.py:29
  34.1 46.9 %collective-permute-start.23 = (f32[128,16]{0,1:T(8,128)S(1)}, f32[128,16]{0,1:T(8,128)}, u32[]{:S(2)}, u32[]{:S(2)}) collective-permute-start(f32[128,16]{0,1:T(8,128)S(1)} %get-tuple-element.49), channel_id=1, source_target_pairs={{0,6},{2,8},{4,10},{6,12},{8,14},{10,0},{12,2},{14,4},{1,7},{3,9},... | collective-permute-start | bytes 24584 | tf_op jit(solution)/shard_map/ppermute | solution.py:29
  34.4 45.4 %collective-permute-start.22 = (f32[128,16]{0,1:T(8,128)S(1)}, f32[128,16]{0,1:T(8,128)}, u32[]{:S(2)}, u32[]{:S(2)}) collective-permute-start(f32[128,16]{0,1:T(8,128)S(1)} %get-tuple-element.49), channel_id=1, source_target_pairs={{0,8},{2,10},{4,12},{6,14},{8,0},{10,2},{12,4},{14,6},{1,9},{3,11}... | collective-permute-start | bytes 24584 | tf_op jit(solution)/shard_map/ppermute | solution.py:29
  35.3 34.6 %collective-permute-start.19 = (f32[128,16]{0,1:T(8,128)S(1)}, f32[128,16]{0,1:T(8,128)}, u32[]{:S(2)}, u32[]{:S(2)}) collective-permute-start(f32[128,16]{0,1:T(8,128)S(1)} %get-tuple-element.49), channel_id=1, source_target_pairs={{0,14},{2,0},{4,2},{6,4},{8,6},{10,8},{12,10},{14,12},{1,15},{3,1}... | collective-permute-start | bytes 24584 | tf_op jit(solution)/shard_map/ppermute | solution.py:29
  43.2 10.0 %copy-start.3 = (bf16[3,3,3,256,128]{4,3,2,1,0:T(8,128)(2,1)S(1)}, bf16[3,3,3,256,128]{4,3,2,1,0:T(8,128)(2,1)}, u32[]{:S(2)}) copy-start(bf16[3,3,3,256,128]{4,3,2,1,0:T(8,128)(2,1)} %rev.3) | copy-start | bytes 5308420
  69.9 101.7 %copy-start.1 = (f32[2,4,16,8,256]{4,0,3,2,1:T(2,128)S(1)}, f32[2,4,16,8,256]{4,0,3,2,1:T(2,128)}, u32[]{:S(2)}) copy-start(f32[2,4,16,8,256]{4,0,3,2,1:T(2,128)} %fusion.21) | copy-start | bytes 3145732
  69.9 3.7 %collective-permute-start.20 = (f32[128,16]{0,1:T(8,128)S(1)}, f32[128,16]{0,1:T(8,128)S(1)}, u32[]{:S(2)}, u32[]{:S(2)}) collective-permute-start(f32[128,16]{0,1:T(8,128)S(1)} %get-tuple-element.49), channel_id=1, source_target_pairs={{0,12},{2,14},{4,0},{6,2},{8,4},{10,6},{12,8},{14,10},{1,13},{3,15... | collective-permute-start | bytes 24584 | tf_op jit(solution)/shard_map/ppermute | solution.py:29
  73.7 4.3 %collective-permute-start.21 = (f32[128,16]{0,1:T(8,128)S(1)}, f32[128,16]{0,1:T(8,128)S(1)}, u32[]{:S(2)}, u32[]{:S(2)}) collective-permute-start(f32[128,16]{0,1:T(8,128)S(1)} %get-tuple-element.49), channel_id=1, source_target_pairs={{0,10},{2,12},{4,14},{6,0},{8,2},{10,4},{12,6},{14,8},{1,11},{3,13... | collective-permute-start | bytes 24584 | tf_op jit(solution)/shard_map/ppermute | solution.py:29
  78.0 22.9 %collective-permute-start.1 = (bf16[2,4,16,128]{3,2,1,0:T(8,128)(2,1)}, bf16[2,4,16,128]{3,2,1,0:T(8,128)(2,1)S(1)}, u32[]{:S(2)}, u32[]{:S(2)}) collective-permute-start(bf16[2,4,16,128]{3,2,1,0:T(8,128)(2,1)} %reshape.138), channel_id=1, source_target_pairs={{0,4},{4,0},{8,12},{12,8},{1,5},{5,1},{9,13},{13,9},{2,6},{6,2},{1... | collective-permute-start | bytes 98312 | tf_op jit(solution)/shard_map/ppermute | solution.py:72
  79.8 35.7 %collective-permute-start.5 = (f32[864,128]{1,0:T(8,128)}, f32[864,128]{1,0:T(8,128)S(1)}, u32[]{:S(2)}, u32[]{:S(2)}) collective-permute-start(f32[864,128]{1,0:T(8,128)} %get-tuple-element.36), channel_id=1, source_target_pairs={{0,2},{2,4},{4,6},{6,8},{8,10},{10,12},{12,14},{14,0},{1,3},{3,5},... | collective-permute-start | bytes 1327112 | tf_op jit(solution)/shard_map/ppermute | solution.py:43
  81.1 45.9 %collective-permute-start.11 = (f32[864,128]{1,0:T(8,128)}, f32[864,128]{1,0:T(8,128)S(1)}, u32[]{:S(2)}, u32[]{:S(2)}) collective-permute-start(f32[864,128]{1,0:T(8,128)} %get-tuple-element.37), channel_id=1, source_target_pairs={{0,14},{2,0},{4,2},{6,4},{8,6},{10,8},{12,10},{14,12},{1,15},{3,1}... | collective-permute-start | bytes 1327112 | tf_op jit(solution)/shard_map/ppermute | solution.py:43
  83.8 52.6 %collective-permute-start.10 = (f32[864,128]{1,0:T(8,128)}, f32[864,128]{1,0:T(8,128)S(1)}, u32[]{:S(2)}, u32[]{:S(2)}) collective-permute-start(f32[864,128]{1,0:T(8,128)} %get-tuple-element.38), channel_id=1, source_target_pairs={{0,12},{2,14},{4,0},{6,2},{8,4},{10,6},{12,8},{14,10},{1,13},{3,15... | collective-permute-start | bytes 1327112 | tf_op jit(solution)/shard_map/ppermute | solution.py:43
  86.9 53.4 %collective-permute-start.9 = (f32[864,128]{1,0:T(8,128)}, f32[864,128]{1,0:T(8,128)S(1)}, u32[]{:S(2)}, u32[]{:S(2)}) collective-permute-start(f32[864,128]{1,0:T(8,128)} %get-tuple-element.39), channel_id=1, source_target_pairs={{0,10},{2,12},{4,14},{6,0},{8,2},{10,4},{12,6},{14,8},{1,11},{3,13... | collective-permute-start | bytes 1327112 | tf_op jit(solution)/shard_map/ppermute | solution.py:43
  101.7 13.7 %collective-permute-start.2 = (bf16[4,4,16,128]{3,2,1,0:T(8,128)(2,1)S(1)}, bf16[4,4,16,128]{3,2,1,0:T(8,128)(2,1)S(1)}, u32[]{:S(2)}, u32[]{:S(2)}) collective-permute-start(bf16[4,4,16,128]{3,2,1,0:T(8,128)(2,1)S(1)} %maximum_select_fusion.1), channel_id=1, source_target_pairs={{0,8},{4,12},{8,0},{12,4},{1,9},{5,13},{9,1},{13,5},{2,10},{6,14},... | collective-permute-start | bytes 196616 | tf_op jit(solution)/shard_map/ppermute | solution.py:72
  115.4 24.9 %collective-permute-start.8 = (f32[864,128]{1,0:T(8,128)}, f32[864,128]{1,0:T(8,128)S(1)}, u32[]{:S(2)}, u32[]{:S(2)}) collective-permute-start(f32[864,128]{1,0:T(8,128)} %get-tuple-element.40), channel_id=1, source_target_pairs={{0,8},{2,10},{4,12},{6,14},{8,0},{10,2},{12,4},{14,6},{1,9},{3,11}... | collective-permute-start | bytes 1327112 | tf_op jit(solution)/shard_map/ppermute | solution.py:43
  115.5 40.1 %collective-permute-start.7 = (f32[864,128]{1,0:T(8,128)}, f32[864,128]{1,0:T(8,128)S(1)}, u32[]{:S(2)}, u32[]{:S(2)}) collective-permute-start(f32[864,128]{1,0:T(8,128)} %get-tuple-element.41), channel_id=1, source_target_pairs={{0,6},{2,8},{4,10},{6,12},{8,14},{10,0},{12,2},{14,4},{1,7},{3,9},... | collective-permute-start | bytes 1327112 | tf_op jit(solution)/shard_map/ppermute | solution.py:43
  127.0 30.6 %collective-permute-start.6 = (f32[864,128]{1,0:T(8,128)}, f32[864,128]{1,0:T(8,128)S(1)}, u32[]{:S(2)}, u32[]{:S(2)}) collective-permute-start(f32[864,128]{1,0:T(8,128)} %get-tuple-element.42), channel_id=1, source_target_pairs={{0,4},{2,6},{4,8},{6,10},{8,12},{10,14},{12,0},{14,2},{1,5},{3,7},... | collective-permute-start | bytes 1327112 | tf_op jit(solution)/shard_map/ppermute | solution.py:43
  136.5 33.0 %collective-permute-start.26 = (f32[2,2,16,8,256]{4,0,3,2,1:T(2,128)}, f32[2,2,16,8,256]{4,0,3,2,1:T(2,128)S(1)}, u32[]{:S(2)}, u32[]{:S(2)}) collective-permute-start(f32[2,2,16,8,256]{4,0,3,2,1:T(2,128)} %fusion.8), channel_id=1, source_target_pairs={{2,0},{3,1},{6,4},{7,5},{10,8},{11,9},{14,12},{15,13},{18,16},{19,... | collective-permute-start | bytes 1572872 | tf_op jit(solution)/shard_map/ppermute | solution.py:13
  157.7 60.3 %collective-permute-start.18 = (bf16[864,128]{1,0:T(8,128)(2,1)S(1)}, bf16[864,128]{1,0:T(8,128)(2,1)S(1)}, u32[]{:S(2)}, u32[]{:S(2)}) collective-permute-start(bf16[864,128]{1,0:T(8,128)(2,1)S(1)} %get-tuple-element.35), channel_id=1, source_target_pairs={{0,2},{2,4},{4,6},{6,8},{8,10},{10,12},{12,14},{14,0},{1,3},{3,5},... | collective-permute-start | bytes 663560 | tf_op jit(solution)/shard_map/ppermute | solution.py:29
  166.9 51.1 %collective-permute-start.17 = (bf16[864,128]{1,0:T(8,128)(2,1)S(1)}, bf16[864,128]{1,0:T(8,128)(2,1)S(1)}, u32[]{:S(2)}, u32[]{:S(2)}) collective-permute-start(bf16[864,128]{1,0:T(8,128)(2,1)S(1)} %get-tuple-element.35), channel_id=1, source_target_pairs={{0,4},{2,6},{4,8},{6,10},{8,12},{10,14},{12,0},{14,2},{1,5},{3,7},... | collective-permute-start | bytes 663560 | tf_op jit(solution)/shard_map/ppermute | solution.py:29
  169.0 49.0 %collective-permute-start.16 = (bf16[864,128]{1,0:T(8,128)(2,1)S(1)}, bf16[864,128]{1,0:T(8,128)(2,1)S(1)}, u32[]{:S(2)}, u32[]{:S(2)}) collective-permute-start(bf16[864,128]{1,0:T(8,128)(2,1)S(1)} %get-tuple-element.35), channel_id=1, source_target_pairs={{0,6},{2,8},{4,10},{6,12},{8,14},{10,0},{12,2},{14,4},{1,7},{3,9},... | collective-permute-start | bytes 663560 | tf_op jit(solution)/shard_map/ppermute | solution.py:29
  169.0 48.9 %collective-permute-start.15 = (bf16[864,128]{1,0:T(8,128)(2,1)S(1)}, bf16[864,128]{1,0:T(8,128)(2,1)S(1)}, u32[]{:S(2)}, u32[]{:S(2)}) collective-permute-start(bf16[864,128]{1,0:T(8,128)(2,1)S(1)} %get-tuple-element.35), channel_id=1, source_target_pairs={{0,8},{2,10},{4,12},{6,14},{8,0},{10,2},{12,4},{14,6},{1,9},{3,11}... | collective-permute-start | bytes 663560 | tf_op jit(solution)/shard_map/ppermute | solution.py:29
  169.4 16.2 %collective-permute-start.12 = (bf16[864,128]{1,0:T(8,128)(2,1)S(1)}, bf16[864,128]{1,0:T(8,128)(2,1)S(1)}, u32[]{:S(2)}, u32[]{:S(2)}) collective-permute-start(bf16[864,128]{1,0:T(8,128)(2,1)S(1)} %get-tuple-element.35), channel_id=1, source_target_pairs={{0,14},{2,0},{4,2},{6,4},{8,6},{10,8},{12,10},{14,12},{1,15},{3,1}... | collective-permute-start | bytes 663560 | tf_op jit(solution)/shard_map/ppermute | solution.py:29
  185.7 17.8 %collective-permute-start.13 = (bf16[864,128]{1,0:T(8,128)(2,1)S(1)}, bf16[864,128]{1,0:T(8,128)(2,1)S(1)}, u32[]{:S(2)}, u32[]{:S(2)}) collective-permute-start(bf16[864,128]{1,0:T(8,128)(2,1)S(1)} %get-tuple-element.35), channel_id=1, source_target_pairs={{0,12},{2,14},{4,0},{6,2},{8,4},{10,6},{12,8},{14,10},{1,13},{3,15... | collective-permute-start | bytes 663560 | tf_op jit(solution)/shard_map/ppermute | solution.py:29
  203.5 13.9 %collective-permute-start.14 = (bf16[864,128]{1,0:T(8,128)(2,1)S(1)}, bf16[864,128]{1,0:T(8,128)(2,1)S(1)}, u32[]{:S(2)}, u32[]{:S(2)}) collective-permute-start(bf16[864,128]{1,0:T(8,128)(2,1)S(1)} %get-tuple-element.35), channel_id=1, source_target_pairs={{0,10},{2,12},{4,14},{6,0},{8,2},{10,4},{12,6},{14,8},{1,11},{3,13... | collective-permute-start | bytes 663560 | tf_op jit(solution)/shard_map/ppermute | solution.py:29
  217.4 2.4 %collective-permute-start.27 = (bf16[2,4,16,8,128]{4,0,3,2,1:T(2,128)(2,1)S(1)}, bf16[2,4,16,8,128]{4,0,3,2,1:T(2,128)(2,1)S(1)}, u32[]{:S(2)}, u32[]{:S(2)}) collective-permute-start(bf16[2,4,16,8,128]{4,0,3,2,1:T(2,128)(2,1)S(1)} %constant_dynamic-slice_fusion), channel_id=1, source_target_pairs={{0,1},{1,0},{2,3},{3,2},{4,5},{5,4},{6,7},{7,6},{8,9},{9,8},{10,11... | collective-permute-start | bytes 786440 | tf_op jit(solution)/shard_map/ppermute | solution.py:177

commit v5 on v3

--- a/solution.py
+++ b/solution.py
@@ -61,11 +61,8 @@
     pad_half = KS // 2
     lat_width = proj_weight.shape[1]
     out_half = conv_weight.shape[2]
-    cache_half = shifted(video[:, frames - (KT - 1) :], "tm", 1)
-    whole_now, whole_cache = (
-        lax.all_gather(video, "chan", axis=4, tiled=True),
-        lax.all_gather(cache_half, "chan", axis=4, tiled=True),
-    )
+    whole_now = lax.all_gather(video, "chan", axis=4, tiled=True)
+    whole_cache = shifted(whole_now[:, frames - (KT - 1) :], "tm", 1)
     timed = jnp.concatenate([whole_cache, whole_now], axis=1)
     kernel = conv_weight.reshape(KT, KS, KS, conv_weight.shape[1], out_half)
     space_pad = [(0, 0), (pad_half, pad_half), (pad_half, pad_half)]
@@ -107,7 +104,7 @@
     grad_conv_local = conv3d(timed, dpre5, space_pad, ("CDHWN", "IDHWO", "DHWNC"))
     grad_conv_local = grad_conv_local.reshape(KT * KS * KS, -1, out_half)
     grad_conv_part = lax.psum_scatter(
-        grad_conv_local.astype(jnp.bfloat16), ("cam", "tm"), scatter_dimension=1, tiled=True
+        grad_conv_local, ("cam", "tm"), scatter_dimension=1, tiled=True
     )
     grad_proj = lax.psum(grad_proj_local, ("cam", "tm"))
     flipped = kernel[::-1, ::-1, ::-1]

time: 178 us -> 188 us (1.056)
  waiting for transfers between devices: 72.1 us -> 85.5 us
    reduce_scatter x1, waiting for transfers between devices: 54.7 us -> 68.3 us  [body(): lax.psum_scatter(grad_conv_local, ('cam', 'tm'), scatter_dimension=1, til...]
    all_gather x2 -> x1, blocking collectives: 4.18 us -> 2.18 us  [body(): whole_now = lax.all_gather(video, 'chan', axis=4, tiled=True)]
    unnamed x19 -> x27, local copies, waits for them, and re-layouts: 6.06 us -> 5.24 us
  transfers between devices with their start and end apart: 9 -> 9, of which waited for: 4 -> 4; matrix products, arithmetic and copies ran while one was open for 13% -> 12% of each run, Pallas kernels for 0% -> 0%
where the time goes in v5:
time: 188 us
  waiting for transfers between devices  85.5 us (45%)
  blocking collectives  32.8 us (17%)
  matrix products  29.9 us (16%)
  between operations  14.4 us (8%)
  starting transfers between devices  11.6 us (6%)
  local copies, waits for them, and re-layouts  9.33 us (5%)
  other arithmetic  4.59 us (2%)
    reduce_scatter x1, waiting for transfers between devices, body(): lax.psum_scatter(grad_conv_local, ('cam', 'tm'), scatter_dimension=1, til...  68.3 us
    conv_general_dilated x4, matrix products, conv3d(): lax.conv_general_dilated(lhs, rhs, window_strides=(1, 1, 1), padding=padd...  27.3 us
    psum x1, blocking collectives, body(): grad_proj = lax.psum(grad_proj_local, ('cam', 'tm'))  27 us
    ppermute x4, waiting for transfers between devices, gathered(): other = lax.ppermute(blocks, axis, pairs)  11.2 us
    ppermute x4, starting transfers between devices, gathered(): other = lax.ppermute(blocks, axis, pairs)  6.58 us
    all_gather x1, waiting for transfers between devices, body(): lax.all_gather(grad_conv_part.astype(jnp.bfloat16), ('cam', 'tm'), axis=1...  5.99 us
    unnamed x27, local copies, waits for them, and re-layouts  5.24 us
    ppermute x2, starting transfers between devices, shifted(): return lax.ppermute(shard, axis, pairs)  4.83 us
  transfers between devices with their start and end apart: 9, of which 4 were waited for; matrix products, arithmetic and copies ran while one was open for 12% of the time, Pallas kernels for 0%

profile of v5, /device:TPU:0, one launch (start us, length us, event | category | flops | bytes accessed | tf_op | source)
XLA Modules:
  0.0 188.1 jit_solution(8297969400039595917)
XLA Ops:
  7.2 0.0 copy-start
  7.2 0.0 copy-start.4
  7.2 0.0 copy-start.7
  7.2 0.0 reduce-scatter.2.cloned.1.call-start
  7.3 3.1 %collective-permute-start.3 = (bf16[1,4,16,128]{3,2,1,0:T(8,128)(2,1)}, bf16[1,4,16,128]{3,2,1,0:T(8,128)(2,1)S(1)}, u32[]{:S(2)}, u32[]{:S(2)}) collective-permute-start(bf16[1,4,16,128]{3,2,1,0:T(8,128)(2,1)} %param.15), channel_id=1, source_target_pairs={{0,4},{4,0},{8,12},{12,8},{1,5},{5,1},{9,13},{13,9},{2,6},{6,2},{1... | collective-permute-start | bytes 49160 | tf_op jit(solution)/shard_map/ppermute | solution.py:25
  10.4 1.2 copy.34
  11.6 2.2 %all_gather.6 = bf16[2,4,16,8,256]{4,0,3,2,1:T(2,128)(2,1)S(1)} all-gather(bf16[2,4,16,8,128]{4,0,3,2,1:T(2,128)(2,1)S(1)} %copy.34), channel_id=1, replica_groups=mesh['groups'=2,'cam'=4,'tm'=2,'chan'=2] {'chan'}, dimensions={4}, use_global_device_ids=true | all-gather | bytes 786432 | tf_op jit(solution)/shard_map/all_gather | solution.py:64
  13.8 0.2 slice.43
  13.9 3.5 %collective-permute-start = (bf16[2,2,16,8,256]{4,0,3,2,1:T(2,128)(2,1)S(1)}, bf16[2,2,16,8,256]{4,0,3,2,1:T(2,128)(2,1)S(1)}, u32[]{:S(2)}, u32[]{:S(2)}) collective-permute-start(bf16[2,2,16,8,256]{4,0,3,2,1:T(2,128)(2,1)S(1)} %slice.43), channel_id=1, source_target_pairs={{0,2},{1,3},{4,6},{5,7},{8,10},{9,11},{12,14},{13,15},{16,18},{17,... | collective-permute-start | bytes 786440 | tf_op jit(solution)/shard_map/ppermute | solution.py:13
  17.5 0.2 reduce-window.8
  17.7 0.1 convert_reduce_fusion
  17.8 0.1 select_reduce_fusion.1
  17.9 0.0 copy-start.5
  18.0 0.0 collective-permute-done.3
  18.0 2.7 %collective-permute-start.4 = (bf16[2,4,16,128]{3,2,1,0:T(8,128)(2,1)S(1)}, bf16[2,4,16,128]{3,2,1,0:T(8,128)(2,1)S(1)}, u32[]{:S(2)}, u32[]{:S(2)}) collective-permute-start(bf16[2,4,16,128]{3,2,1,0:T(8,128)(2,1)S(1)} %maximum_select_fusion.5), channel_id=1, source_target_pairs={{0,8},{4,12},{8,0},{12,4},{1,9},{5,13},{9,1},{13,5},{2,10},{6,14},... | collective-permute-start | bytes 98312 | tf_op jit(solution)/shard_map/ppermute | solution.py:25
  20.7 0.2 broadcast_select_fusion
  20.8 2.3 %collective-permute-done.4 = bf16[2,4,16,128]{3,2,1,0:T(8,128)(2,1)S(1)} collective-permute-done((bf16[2,4,16,128]{3,2,1,0:T(8,128)(2,1)S(1)}, bf16[2,4,16,128]{3,2,1,0:T(8,128)(2,1)S(1)}, u32[]{:S(2)}, u32[]{:S(2)}) %collective-permute-start.4) | collective-permute-done | bytes 32800 | tf_op jit(solution)/shard_map/ppermute | solution.py:25
  23.2 0.4 convolution_convert_fusion
  23.6 0.2 reshape.140
  23.8 0.0 collective-permute-done
  23.8 0.2 constant_dynamic-update-slice_fusion.1
  24.0 0.5 constant_dynamic-update-slice_fusion
  24.6 6.6 %fusion.27 = f32[2,4,16,8,128]{4,0,3,2,1:T(2,128)S(1)} fusion(bf16[2,6,16,8,256]{4,0,3,2,1:T(2,128)(2,1)S(1)} %constant_dynamic-update-slice_fusion, bf16[3,3,3,256,128]{4,3,2,1,0:T(8,128)(2,1)S(1)} %bitcast.75), kind=kOutput, calls=%fused_computation.55 | convolution fusion | flops 1591738368 | bytes 3080192 | tf_op jit(solution)/shard_map/conv_general_dilated | solution.py:37
  31.1 0.9 multiply_convert_fusion
  32.0 0.2 fusion.5
  32.2 0.0 copy-done
  32.2 0.2 fusion.1
  32.4 10.6 %fusion.25 = f32[3,3,3,256,128]{4,3,2,1,0:T(8,128)} fusion(bf16[2,6,16,8,256]{4,0,3,2,1:T(2,128)(2,1)S(1)} %constant_dynamic-update-slice_fusion, bf16[2,4,16,8,128]{4,3,2,1,0:T(8,128)(2,1)S(1)} %bitcast.79), kind=kOutput, calls=%fused_computation.53 | convolution fusion | flops 1591738368 | bytes 4587520 | tf_op jit(solution)/shard_map/conv_general_dilated | solution.py:37
  43.0 0.0 reduce-scatter.2.cloned.1.call-update
  43.1 0.0 all-gather.2.cloned.1.call-start
  43.1 1.4 rev.3
  44.5 1.0 copy.38
  45.5 0.2 fusion.28
  45.7 3.6 %psum.14 = bf16[1024,16]{0,1:T(8,128)(2,1)S(1)} all-reduce(f32[1024,16]{0,1:T(8,128)S(1)} %fusion.28), channel_id=1, replica_groups=mesh['groups'=2,'cam'=4,'tm'=2,'chan'=2] {'chan'}, use_global_device_ids=true, to_apply=%region_4.5 | all-reduce | flops 16384 | bytes 98304 | tf_op jit(solution)/shard_map/psum | solution.py:74
  49.3 0.2 copy.36
  49.5 0.2 reshape.138
  49.7 0.3 collective-permute-start.1
  50.0 5.9 %fusion.23 = f32[2,4,16,8,256]{4,0,3,2,1:T(2,128)S(1)} fusion(bf16[3,3,3,256,128]{4,3,2,1,0:T(8,128)(2,1)S(1)} %bitcast.77, bf16[2,4,16,8,128]{4,3,2,1,0:T(8,128)(2,1)} %bitcast.81), kind=kOutput, calls=%fused_computation.51 | convolution fusion | flops 1193803776 | bytes 3080192 | tf_op jit(solution)/shard_map/conv_general_dilated | solution.py:37
  55.9 68.3 %reduce-scatter.2.cloned.1.call-done = f32[27,32,128]{2,1,0:T(8,128)} async-done(((f32[27,256,128]{2,1,0:T(8,128)}), f32[27,32,128]{2,1,0:T(8,128)}) %reduce-scatter.2.cloned.1.call-update) | async-done | bytes 442384 | tf_op jit(solution)/shard_map/reduce_scatter | solution.py:106
  124.2 1.7 convert_element_type.50
  125.9 0.0 all-gather.2.cloned.1.call-update
  125.9 0.0 copy-start.2
  125.9 4.2 %fusion.8 = f32[2,2,16,8,256]{4,0,3,2,1:T(2,128)S(1)} fusion(bf16[3,3,3,256,128]{4,3,2,1,0:T(8,128)(2,1)} %rev.3, bf16[2,4,16,8,128]{4,0,3,2,1:T(2,128)(2,1)} %copy.38), kind=kOutput, calls=%fused_computation.16 | convolution fusion | flops 397934592 | bytes 2424832 | tf_op jit(solution)/shard_map/conv_general_dilated | solution.py:37
  130.2 0.2 fusion.29
  130.4 0.3 concatenate.62
  130.7 1.3 collective-permute-start.5
  132.0 27.0 %psum.15 = f32[128,16]{0,1:T(8,128)} all-reduce(f32[128,16]{0,1:T(8,128)S(1)} %fusion.29), channel_id=1, replica_groups=mesh['groups'=2,'cam'=4,'tm'=2,'chan'=2] {'cam','tm'}, use_global_device_ids=true, to_apply=%region_6.7 | all-reduce | flops 2048 | bytes 16384 | tf_op jit(solution)/shard_map/psum | solution.py:109
  159.0 0.0 collective-permute-done.1
  159.0 0.5 collective-permute-start.2
  159.6 0.1 maximum_select_fusion.2
  159.7 8.9 %collective-permute-done.2 = bf16[4,4,16,128]{3,2,1,0:T(8,128)(2,1)S(1)} collective-permute-done((bf16[4,4,16,128]{3,2,1,0:T(8,128)(2,1)S(1)}, bf16[4,4,16,128]{3,2,1,0:T(8,128)(2,1)S(1)}, u32[]{:S(2)}, u32[]{:S(2)}) %collective-permute-start.2) | collective-permute-done | bytes 65568 | tf_op jit(solution)/shard_map/ppermute | solution.py:25
  168.6 0.1 copy.62
  168.7 0.0 collective-permute-done.5
  168.7 0.3 fusion.2
  169.0 0.4 convert_element_type.53
  169.4 0.2 constant_dynamic-slice_fusion
  169.6 0.1 collective-permute-start.6
  169.7 0.1 maximum_select_fusion
  169.8 1.6 fusion.20
  171.4 0.0 collective-permute-done.6
  171.4 0.3 add_convert_fusion
  171.7 0.7 copy.43
  172.4 6.0 %all-gather.2.cloned.1.call-done = bf16[27,256,128]{2,1,0:T(8,128)(2,1)} async-done(((bf16[27,32,128]{2,1,0:T(8,128)(2,1)}), bf16[27,256,128]{2,1,0:T(8,128)(2,1)}) %all-gather.2.cloned.1.call-update) | async-done | bytes 1769488 | tf_op jit(solution)/shard_map/all_gather | solution.py:131
  178.4 2.9 %copy.70 = bf16[27,256,128]{2,1,0:T(8,128)(2,1)} copy(bf16[27,256,128]{2,1,0:T(8,128)(2,1)} %all-gather.2.cloned.1.call-done) | data formatting | bytes 3538944
  (20 shorter events, 0.2 us)
Async XLA Ops:
  7.2 25.1 %copy-start = (bf16[128,16]{0,1:T(8,128)(2,1)S(1)}, bf16[128,16]{0,1:T(8,128)(2,1)}, u32[]{:S(2)}) copy-start(bf16[128,16]{0,1:T(8,128)(2,1)} %param.11) | copy-start | bytes 12292
  7.2 10.7 %copy-start.4 = (bf16[1,4,16,128]{3,2,1,0:T(8,128)(2,1)S(1)}, bf16[1,4,16,128]{3,2,1,0:T(8,128)(2,1)}, u32[]{:S(2)}) copy-start(bf16[1,4,16,128]{3,2,1,0:T(8,128)(2,1)} %param.15) | copy-start | bytes 49156
  7.2 10.3 %copy-start.7 = (s32[4]{0:T(128)S(1)}, s32[4]{0:T(128)}, u32[]{:S(2)}) copy-start(s32[4]{0:T(128)} %param.12) | copy-start | bytes 52
  7.2 10.5 %copy-start.8 = (s32[8]{0:T(128)S(1)}, s32[8]{0:T(128)}, u32[]{:S(2)}) copy-start(s32[8]{0:T(128)} %param.13) | copy-start | bytes 100
  7.2 10.6 %copy-start.6 = (s32[4]{0:T(128)S(1)}, s32[4]{0:T(128)}, u32[]{:S(2)}) copy-start(s32[4]{0:T(128)} %param.14) | copy-start | bytes 52
  7.2 117.0 %reduce-scatter.2.cloned.1.call-start = ((), (), s32[]{:S(2)}) async-start(), calls=%async_computation.1 | async-start | bytes 3981312 | tf_op jit(solution)/shard_map/reduce_scatter | solution.py:106
  7.3 10.7 %collective-permute-start.3 = (bf16[1,4,16,128]{3,2,1,0:T(8,128)(2,1)}, bf16[1,4,16,128]{3,2,1,0:T(8,128)(2,1)S(1)}, u32[]{:S(2)}, u32[]{:S(2)}) collective-permute-start(bf16[1,4,16,128]{3,2,1,0:T(8,128)(2,1)} %param.15), channel_id=1, source_target_pairs={{0,4},{4,0},{8,12},{12,8},{1,5},{5,1},{9,13},{13,9},{2,6},{6,2},{1... | collective-permute-start | bytes 49160 | tf_op jit(solution)/shard_map/ppermute | solution.py:25
  13.8 10.8 %copy-start.1 = (bf16[27,256,128]{2,1,0:T(8,128)(2,1)S(1)}, bf16[27,256,128]{2,1,0:T(8,128)(2,1)}, u32[]{:S(2)}) copy-start(bf16[27,256,128]{2,1,0:T(8,128)(2,1)} %param.10) | copy-start | bytes 5308420
  13.9 9.9 %collective-permute-start = (bf16[2,2,16,8,256]{4,0,3,2,1:T(2,128)(2,1)S(1)}, bf16[2,2,16,8,256]{4,0,3,2,1:T(2,128)(2,1)S(1)}, u32[]{:S(2)}, u32[]{:S(2)}) collective-permute-start(bf16[2,2,16,8,256]{4,0,3,2,1:T(2,128)(2,1)S(1)} %slice.43), channel_id=1, source_target_pairs={{0,2},{1,3},{4,6},{5,7},{8,10},{9,11},{12,14},{13,15},{16,18},{17,... | collective-permute-start | bytes 786440 | tf_op jit(solution)/shard_map/ppermute | solution.py:13
  17.9 5.3 %copy-start.5 = (f32[4,8]{1,0:T(4,128)}, f32[4,8]{1,0:T(4,128)S(1)}, u32[]{:S(2)}) copy-start(f32[4,8]{1,0:T(4,128)S(1)} %fusion.17) | copy-start | bytes 388
  18.0 5.1 %collective-permute-start.4 = (bf16[2,4,16,128]{3,2,1,0:T(8,128)(2,1)S(1)}, bf16[2,4,16,128]{3,2,1,0:T(8,128)(2,1)S(1)}, u32[]{:S(2)}, u32[]{:S(2)}) collective-permute-start(bf16[2,4,16,128]{3,2,1,0:T(8,128)(2,1)S(1)} %maximum_select_fusion.5), channel_id=1, source_target_pairs={{0,8},{4,12},{8,0},{12,4},{1,9},{5,13},{9,1},{13,5},{2,10},{6,14},... | collective-permute-start | bytes 98312 | tf_op jit(solution)/shard_map/ppermute | solution.py:25
  32.4 12.1 %copy-start.3 = (bf16[1024,128]{1,0:T(8,128)(2,1)}, bf16[1024,128]{1,0:T(8,128)(2,1)S(1)}, u32[]{:S(2)}) copy-start(bf16[1024,128]{1,0:T(8,128)(2,1)S(1)} %fusion.1) | copy-start | bytes 786436
  43.1 135.3 %all-gather.2.cloned.1.call-start = ((), (), s32[]{:S(2)}) async-start(), calls=%async_computation.2 | async-start | bytes 1990656 | tf_op jit(solution)/shard_map/all_gather | solution.py:131
  49.7 109.3 %collective-permute-start.1 = (bf16[2,4,16,128]{3,2,1,0:T(8,128)(2,1)S(1)}, bf16[2,4,16,128]{3,2,1,0:T(8,128)(2,1)S(1)}, u32[]{:S(2)}, u32[]{:S(2)}) collective-permute-start(bf16[2,4,16,128]{3,2,1,0:T(8,128)(2,1)S(1)} %reshape.138), channel_id=1, source_target_pairs={{0,4},{4,0},{8,12},{12,8},{1,5},{5,1},{9,13},{13,9},{2,6},{6,2},{1... | collective-permute-start | bytes 98312 | tf_op jit(solution)/shard_map/ppermute | solution.py:25
  125.9 4.2 %copy-start.2 = (bf16[2,4,16,8,128]{4,3,2,1,0:T(8,128)(2,1)S(1)}, bf16[2,4,16,8,128]{4,3,2,1,0:T(8,128)(2,1)}, u32[]{:S(2)}) copy-start(bf16[2,4,16,8,128]{4,3,2,1,0:T(8,128)(2,1)} %get-tuple-element.34) | copy-start | bytes 786436
  130.7 38.0 %collective-permute-start.5 = (f32[2,2,16,8,256]{4,0,3,2,1:T(2,128)S(1)}, f32[2,2,16,8,256]{4,0,3,2,1:T(2,128)S(1)}, u32[]{:S(2)}, u32[]{:S(2)}) collective-permute-start(f32[2,2,16,8,256]{4,0,3,2,1:T(2,128)S(1)} %fusion.8), channel_id=1, source_target_pairs={{2,0},{3,1},{6,4},{7,5},{10,8},{11,9},{14,12},{15,13},{18,16},{19,... | collective-permute-start | bytes 1572872 | tf_op jit(solution)/shard_map/ppermute | solution.py:13
  159.0 9.6 %collective-permute-start.2 = (bf16[4,4,16,128]{3,2,1,0:T(8,128)(2,1)S(1)}, bf16[4,4,16,128]{3,2,1,0:T(8,128)(2,1)S(1)}, u32[]{:S(2)}, u32[]{:S(2)}) collective-permute-start(bf16[4,4,16,128]{3,2,1,0:T(8,128)(2,1)S(1)} %maximum_select_fusion.1), channel_id=1, source_target_pairs={{0,8},{4,12},{8,0},{12,4},{1,9},{5,13},{9,1},{13,5},{2,10},{6,14},... | collective-permute-start | bytes 196616 | tf_op jit(solution)/shard_map/ppermute | solution.py:25
  169.6 1.8 collective-permute-start.6
Sparse Core Ops, SparseCore 0:
  43.2 80.9 reduce-scatter.1
  126.2 52.1 all-gather.1
